TPU v7x, 256 devices: a whole 4x4x8 slice. The times are simulated.
256 devices in a mesh: ctx: 32 (over z, x_lo, core), heads: 8 (over x_hi, y).
Axes of the slice: x: 4 (x_hi: 2, x_lo: 2; x = x_hi * 2 + x_lo), y: 4, z: 8, core: 2. Of those that a mesh axis runs over, the one named last changes fastest.
Arguments:
- hidden: bfloat16 [16384, 5376], P(('ctx', 'heads')), may hold values from -8 to 8
- query_weight: bfloat16 [5376, 2048], P(None, 'heads'), may hold values from -0.5 to 0.5
- key_weight: bfloat16 [5376, 1024], P(None, 'heads'), may hold values from -0.5 to 0.5
- value_weight: bfloat16 [5376, 1024], P(None, 'heads'), may hold values from -0.078125 to 0.078125
- query_gain: float32 [128], replicated, may hold values from 0.5 to 6
- key_gain: float32 [128], replicated, may hold values from 0.5 to 6
- out_grad: bfloat16 [16384, 2048], P('ctx', 'heads'), may hold values from -6 to 6
Outputs:
- attention: bfloat16 [16384, 2048], P('ctx', 'heads')
- input_grad: bfloat16 [16384, 5376], P(('ctx', 'heads'))
- query_weight_grad: float32 [5376, 2048], P('ctx', 'heads')
- key_weight_grad: float32 [5376, 1024], P('ctx', 'heads')
- value_weight_grad: float32 [5376, 1024], P('ctx', 'heads')
All inputs are finite; a program needn't handle non-finite values.
Results may differ from a plain program's by a relative error of at most 0.039.
Values may be sent and summed in bfloat16 or wider, within the bound.
No kernel may reach another device: no remote copies, remote signals or barrier semaphores. Data moves between devices by JAX's collectives and lax.ppermute only.
A program may use at most 128 MiB of HBM per device.

v0:
```python
import math

import jax
import jax.numpy as jnp
from jax import lax
from jax.sharding import PartitionSpec as P

HEAD_DIM = 128
WINDOW = 1024
SCALAR = 168
HEADS = 16
KV_HEADS = 8


def passed_along(block, axis, distance):
    devices = range(lax.axis_size(axis))
    route = [(i - distance, i) for i in devices if i - distance in devices]
    return lax.ppermute(block, axis, route)


def rope_tables(positions, head_size):
    half_size = head_size // 2
    indices = jnp.arange(half_size, dtype=jnp.float32)
    inverse = jnp.exp(indices * (-2.0 * math.log(10000.0) / head_size))
    angles = positions.astype(jnp.float32)[:, None] * inverse[None, :]
    return (jnp.cos(angles), jnp.sin(angles))


def prepare(projected, cosine, sine_table, channel_gain, factor):
    row_count = projected.shape[0]
    head_size = channel_gain.shape[0]
    pieces = projected.reshape(row_count, -1, head_size)
    normed = (
        pieces * lax.rsqrt(jnp.mean(pieces * pieces, axis=-1, keepdims=True) + 1e-06) * channel_gain
    )
    half_size = head_size // 2
    leading = normed[..., :half_size]
    trailing = normed[..., half_size:]
    cos_rows = cosine[:, None, :]
    sin_rows = sine_table[:, None, :]
    turned = jnp.concatenate(
        [leading * cos_rows - trailing * sin_rows, trailing * cos_rows + leading * sin_rows],
        axis=-1,
    )
    return (turned * factor).reshape(row_count, -1)


def band_mask(query_pos, key_pos):
    separation = query_pos[:, None] - key_pos[None, :]
    return (separation >= 0) & (separation < WINDOW) & (key_pos[None, :] >= 0)


def head_grids(query_block, key_window, value_window, group_size):
    query_grid = query_block.reshape(query_block.shape[0], -1, group_size, HEAD_DIM)
    key_grid = key_window.reshape(key_window.shape[0], -1, HEAD_DIM)
    value_grid = value_window.reshape(value_window.shape[0], -1, HEAD_DIM)
    return (query_grid, key_grid, value_grid)


def attend_forward(query_block, key_window, value_window, allowed, group_size):
    query_grid, key_grid, value_grid = head_grids(query_block, key_window, value_window, group_size)
    scores = jnp.einsum("qkgd,jkd->kgqj", query_grid, key_grid, preferred_element_type=jnp.float32)
    masked = jnp.where(allowed, scores, -1e30)
    highest = jnp.max(masked, axis=-1, keepdims=True)
    total = jnp.sum(jnp.exp(masked - highest), axis=-1, keepdims=True)
    log_total = highest + jnp.log(total)
    weights = jnp.where(allowed, jnp.exp(masked - log_total), 0.0)
    output = jnp.einsum(
        "kgqj,jkd->qkgd",
        weights.astype(jnp.bfloat16),
        value_grid,
        preferred_element_type=jnp.float32,
    )
    return (output.reshape(query_block.shape[0], -1), log_total[..., 0])


def attend_backward(
    query_block,
    key_window,
    value_window,
    allowed,
    log_total,
    out_block,
    attention_block,
    group_size,
):
    query_grid, key_grid, value_grid = head_grids(query_block, key_window, value_window, group_size)
    row_count = query_block.shape[0]
    grad_grid = out_block.reshape(row_count, -1, group_size, HEAD_DIM)
    attention_grid = attention_block.reshape(row_count, -1, group_size, HEAD_DIM)
    scores = jnp.einsum("qkgd,jkd->kgqj", query_grid, key_grid, preferred_element_type=jnp.float32)
    masked = jnp.where(allowed, scores, -1e30)
    weights = jnp.where(allowed, jnp.exp(masked - log_total[..., None]), 0.0)
    delta = jnp.einsum(
        "qkgd,qkgd->kgq", grad_grid, attention_grid, preferred_element_type=jnp.float32
    )
    products = jnp.einsum(
        "qkgd,jkd->kgqj", grad_grid, value_grid, preferred_element_type=jnp.float32
    )
    shifts = (weights * (products - delta[..., None])).astype(jnp.bfloat16)
    query_cot = jnp.einsum(
        "kgqj,jkd->qkgd", shifts, key_grid, preferred_element_type=jnp.float32
    ).reshape(row_count, -1)
    key_cot = jnp.einsum(
        "kgqj,qkgd->jkd", shifts, query_grid, preferred_element_type=jnp.float32
    ).reshape(key_window.shape[0], -1)
    value_cot = jnp.einsum(
        "kgqj,qkgd->jkd",
        weights.astype(jnp.bfloat16),
        grad_grid,
        preferred_element_type=jnp.float32,
    ).reshape(key_window.shape[0], -1)
    return (query_cot, key_cot, value_cot)


def per_device(hidden, query_weight, key_weight, value_weight, query_gain, key_gain, out_grad):
    token_count = out_grad.shape[0]
    group_size = HEADS // KV_HEADS
    block_rows = min(token_count, 512)
    block_count = token_count // block_rows
    window_rows = block_rows + WINDOW
    reach_blocks = (WINDOW - 2) // token_count + 1
    position_base = lax.axis_index("ctx") * token_count
    gathered = lax.all_gather(hidden, "heads", axis=0, tiled=True)
    query_proj = jnp.dot(gathered, query_weight, preferred_element_type=jnp.float32)
    key_proj = jnp.dot(gathered, key_weight, preferred_element_type=jnp.float32)
    value_proj = jnp.dot(gathered, value_weight, preferred_element_type=jnp.float32)
    positions = position_base + jnp.arange(token_count, dtype=jnp.int32)
    cosine, sine_table = rope_tables(positions, HEAD_DIM)
    query_full, query_back = jax.vjp(
        lambda projected: prepare(projected, cosine, sine_table, query_gain, SCALAR ** (-0.5)),
        query_proj,
    )
    key_full, key_back = jax.vjp(
        lambda projected: prepare(projected, cosine, sine_table, key_gain, 1.0), key_proj
    )
    query_cast = query_full.astype(jnp.bfloat16)
    key_value = jnp.stack([key_full.astype(jnp.bfloat16), value_proj.astype(jnp.bfloat16)])
    received = [passed_along(key_value, "ctx", distance) for distance in range(1, reach_blocks + 1)]
    window_pair = jnp.concatenate(received[::-1] + [key_value], axis=1)
    key_span = window_pair[0]
    value_span = window_pair[1]

    def window_of(block_index):
        block_start = block_index * block_rows
        query_pos = position_base + block_start + jnp.arange(block_rows, dtype=jnp.int32)
        key_pos = position_base - WINDOW + block_start + jnp.arange(window_rows, dtype=jnp.int32)
        return (query_cast, key_span, value_span, band_mask(query_pos, key_pos))

    def forward_block(block_index):
        query_block, key_window, value_window, allowed = window_of(block_index)
        return attend_forward(query_block, key_window, value_window, allowed, group_size)

    outputs, log_totals = lax.map(forward_block, jnp.arange(block_count, dtype=jnp.int32))
    attention = outputs.reshape(token_count, -1).astype(jnp.bfloat16)

    def backward_block(block_index, carry):
        query_acc, pair_acc = carry
        query_block, key_window, value_window, allowed = window_of(block_index)
        block_start = block_index * block_rows
        query_cot, key_cot, value_cot = attend_backward(
            query_block,
            key_window,
            value_window,
            allowed,
            log_totals[block_index],
            out_grad,
            attention,
            group_size,
        )
        query_acc = query_cot
        region = pair_acc + jnp.stack([key_cot, value_cot])
        pair_acc = region
        return (query_acc, pair_acc)

    query_zero = jnp.zeros((token_count, query_weight.shape[1]), jnp.float32)
    pair_zero = jnp.zeros((2, (reach_blocks + 1) * token_count, key_weight.shape[1]), jnp.float32)
    query_acc, pair_acc = lax.fori_loop(0, block_count, backward_block, (query_zero, pair_zero))
    grad_query = query_back(query_acc)[0].astype(jnp.bfloat16)
    grad_scale = float(lax.axis_size("ctx") * token_count) ** (-0.5)
    contract = (((0,), (0,)), ((), ()))
    own_pair = pair_acc[:, reach_blocks * token_count :]
    for distance in range(1, reach_blocks + 1):
        lower_row = (reach_blocks - distance) * token_count
        own_pair = own_pair + passed_along(
            pair_acc[:, lower_row : lower_row + token_count], "ctx", -distance
        )
    grad_key = key_back(own_pair[0])[0].astype(jnp.bfloat16)
    grad_value = own_pair[1].astype(jnp.bfloat16)
    key_width = key_weight.shape[1]
    query_width = query_weight.shape[1]
    summed = lax.psum_scatter(
        (
            lax.dot_general(
                gathered,
                jnp.concatenate([grad_query, grad_key, grad_value], axis=1),
                contract,
                preferred_element_type=jnp.float32,
            )
            * grad_scale
        ).astype(jnp.bfloat16),
        "ctx",
        scatter_dimension=0,
        tiled=True,
    ).astype(jnp.float32)
    query_weight_grad = summed[:, :query_width]
    key_weight_grad = summed[:, query_width : query_width + key_width]
    value_weight_grad = summed[:, query_width + key_width :]
    back_contract = (((1,), (1,)), ((), ()))
    partial_sum = lax.dot_general(
        grad_query, query_weight, back_contract, preferred_element_type=jnp.float32
    )
    partial_sum = partial_sum + lax.dot_general(
        grad_key, key_weight, back_contract, preferred_element_type=jnp.float32
    )
    input_grad = lax.psum_scatter(
        (
            partial_sum
            + lax.dot_general(
                grad_value, value_weight, back_contract, preferred_element_type=jnp.float32
            )
        ).astype(jnp.bfloat16),
        "heads",
        scatter_dimension=0,
        tiled=True,
    )
    return (attention, input_grad, query_weight_grad, key_weight_grad, value_weight_grad)


def solution(mesh):
    return jax.shard_map(
        per_device,
        mesh=mesh,
        in_specs=(
            P(("ctx", "heads"), None),
            P(None, "heads"),
            P(None, "heads"),
            P(None, "heads"),
            P(),
            P(),
            P("ctx", "heads"),
        ),
        out_specs=(
            P("ctx", "heads"),
            P(("ctx", "heads"), None),
            P("ctx", "heads"),
            P("ctx", "heads"),
            P("ctx", "heads"),
        ),
        check_vma=False,
    )
```

profile of v0, /device:TPU:96, one launch (start us, length us, event | category | flops | bytes accessed | tf_op | source)
XLA Modules:
  0.0 426.3 jit_solution(6690216470228752549)
XLA Ops:
  7.2 0.0 all-gather.2.cloned.1.call-start
  7.2 0.7 all-gather.2.cloned.1.call-update
  7.9 0.0 reduce-scatter.7.cloned.1.call-start
  8.0 1.1 reshape.322
  9.0 0.9 copy.65
  10.0 1.8 multiply_cosine_fusion
  11.8 1.9 fusion.8
  13.7 85.8 %all-gather.2.cloned.1.call-done = bf16[512,5376]{1,0:T(8,128)(2,1)} async-done(((bf16[64,5376]{1,0:T(8,128)(2,1)}), bf16[512,5376]{1,0:T(8,128)(2,1)}) %all-gather.2.cloned.1.call-update) | async-done | bytes 5505040 | tf_op jit(solution)/shard_map/all_gather | solution.py:124
  99.6 5.1 %multiply_reduce_fusion.3 = (f32[512]{0:T(512)S(1)}, f32[512,128]{0,1:T(8,128)S(1)}) fusion(bf16[512,5376]{1,0:T(8,128)(2,1)} %all-gather.2.cloned.1.call-done, bf16[5376,128]{1,0:T(8,128)(2,1)} %param.9), kind=kOutput, calls=%fused_computation.67 | convolution fusion | flops 704773632 | bytes 7145472 | tf_op jit(solution)/shard_map/dot_general | solution.py:126
  104.7 0.1 multiply_bitcast_fusion
  104.8 0.6 fusion.34
  105.4 2.0 fusion.10
  107.4 0.6 copy-done.16
  108.0 0.7 pad_maximum_fusion.1
  108.7 1.9 collective-permute-start.1
  110.7 2.7 collective-permute-start
  113.3 3.0 multiply_reduce_fusion.2
  116.4 1.2 copy.52
  117.6 0.8 fusion.41
  118.4 0.9 multiply_multiply_fusion
  119.2 1.2 multiply_subtract_fusion
  120.5 0.2 fusion.16
  120.7 2.2 collective-permute-done
  122.9 1.2 maximum_maximum_fusion
  124.2 1.2 fusion.3
  125.4 1.2 exponential_reduce_fusion
  126.7 2.9 bitcast_convert_fusion
  129.6 3.1 convolution_bitcast_fusion
  132.7 2.1 copy.79
  134.8 2.4 multiply_reduce_fusion
  137.2 1.7 copy.80
  138.9 5.5 %fusion.5 = bf16[2,512,1536]{1,2,0:T(8,128)(2,1)S(1)} fusion(bf16[512,2,128]{0,2,1:T(8,128)(2,1)} %copy.65, f32[1536,512,2]{1,0,2:T(8,128)} %copy-done.2, f32[2,512]{1,0:T(2,128)} %copy.80, f32[2,512]{1,0:T(2,128)} %copy-done.28, pred[512,1536]{0,1:T(8,128)(4,1)} %fusion.8, bf16[2,1536,128]{1,2,0:T(8,128)(2,1)} %copy-done.8), kind=kOutput, calls=%fused_computation.13 | convolution fusion | flops 412090368 | bytes 10887168 | tf_op jit(solution)/shard_map/while/body/eval_jaxpr/qkgd,jkd->kgqj/dot_general | solution.py:97
  144.4 1.6 fusion.9
  146.1 1.2 convolution_bitcast_fusion.1
  147.3 0.3 multiply_add_fusion.1
  147.5 0.6 copy-done.3
  148.1 1.1 fusion.12
  149.2 2.1 collective-permute-start.2
  151.3 3.4 collective-permute-start.3
  154.7 0.4 multiply_reduce_fusion.1
  155.1 1.2 fusion.11
  156.3 1.8 copy.61
  158.1 3.4 collective-permute-done.2
  161.5 11.2 %collective-permute-done.3 = f32[2,512,128]{1,2,0:T(8,128)} collective-permute-done((f32[2,512,128]{1,2,0:T(8,128)}, f32[2,512,128]{1,2,0:T(8,128)}, u32[]{:S(2)}, u32[]{:S(2)}) %collective-permute-start.3) | collective-permute-done | bytes 524320 | tf_op jit(solution)/shard_map/ppermute | solution.py:18
  172.8 1.5 fusion.15
  174.3 1.2 fusion.37
  175.5 0.8 fusion.24
  176.3 0.8 fusion.40
  177.1 0.6 copy-done.20
  177.7 7.7 %fusion = bf16[5376,512]{0,1:T(8,128)(2,1)} fusion(bf16[512,5376]{1,0:T(8,128)(2,1)} %all-gather.2.cloned.1.call-done, bf16[512,128]{0,1:T(8,128)(2,1)S(1)} %fusion.39, bf16[512,128]{0,1:T(8,128)(2,1)S(1)} %fusion.40, bf16[512,256]{0,1:T(8,128)(2,1)S(1)} %bitcast.138), kind=kOutput, calls=%fused_computation.2 | convolution fusion | flops 2825650176 | bytes 11534336 | tf_op jit(solution)/shard_map/dot_general | solution.py:194
  185.4 8.3 %copy.88 = bf16[5376,512]{1,0:T(8,128)(2,1)} copy(bf16[5376,512]{0,1:T(8,128)(2,1)} %fusion) | data formatting | bytes 11010048
  193.8 0.0 reduce-scatter.5.cloned.1.call-start
  193.8 0.9 copy-done.19
  194.7 5.9 %fusion.49 = f32[512,5376]{1,0:T(8,128)} fusion(bf16[512,256]{0,1:T(8,128)(2,1)S(1)} %bitcast.139, bf16[5376,256]{1,0:T(8,128)(2,1)S(1)} %copy-done), kind=kOutput, calls=%fused_computation.101 | convolution fusion | flops 1409286144 | bytes 14024704 | tf_op jit(solution)/shard_map/dot_general | solution.py:210
  200.6 5.7 %fusion.50 = f32[512,5376]{1,0:T(8,128)} fusion(bf16[512,128]{0,1:T(8,128)(2,1)S(1)} %copy-done.21, bf16[5376,128]{1,0:T(8,128)(2,1)S(1)} %copy-done.7), kind=kOutput, calls=%fused_computation.102 | convolution fusion | flops 704643072 | bytes 12517376 | tf_op jit(solution)/shard_map/dot_general | solution.py:213
  206.3 11.4 %add_convert_fusion = bf16[512,5376]{1,0:T(8,128)(2,1)} fusion(f32[512,5376]{1,0:T(8,128)} %fusion.49, f32[512,5376]{1,0:T(8,128)} %fusion.50, bf16[5376,128]{1,0:T(8,128)(2,1)S(1)} %copy-done.6, f32[2,512,128]{1,2,0:T(8,128)S(1)} %fusion.15), kind=kOutput, calls=%fused_computation.1 | convolution fusion | flops 712900608 | bytes 29032448 | tf_op jit(solution)/shard_map/dot_general | solution.py:219
  217.7 0.9 copy-done.22
  218.6 0.8 copy.66
  219.5 92.5 %reduce-scatter.7.cloned.1.call-done = bf16[168,512]{1,0:T(8,128)(2,1)} async-done(((bf16[5376,512]{1,0:T(8,128)(2,1)}), bf16[168,512]{1,0:T(8,128)(2,1)}) %reduce-scatter.7.cloned.1.call-update) | async-done | bytes 172048
  312.0 1.0 copy.89
  313.0 0.8 copy.67
  313.8 0.7 copy.69
  314.6 0.7 copy.68
  315.3 104.5 %reduce-scatter.5.cloned.1.call-done = bf16[64,5376]{1,0:T(8,128)(2,1)} async-done(((bf16[512,5376]{1,0:T(8,128)(2,1)}), bf16[64,5376]{1,0:T(8,128)(2,1)}) %reduce-scatter.5.cloned.1.call-update) | async-done | bytes 688144 | tf_op jit(solution)/shard_map/reduce_scatter | solution.py:216
  (70 shorter events, 0.3 us)
Async XLA Ops:
  7.2 106.2 %copy-start = (bf16[5376,256]{1,0:T(8,128)(2,1)S(1)}, bf16[5376,256]{1,0:T(8,128)(2,1)}, u32[]{:S(2)}) copy-start(bf16[5376,256]{1,0:T(8,128)(2,1)} %param.8) | copy-start | bytes 8257540
  7.2 92.4 %all-gather.2.cloned.1.call-start = ((), (), s32[]{:S(2)}) async-start(), calls=%async_computation.2 | async-start | bytes 6193152 | tf_op jit(solution)/shard_map/all_gather | solution.py:124
  7.9 304.0 %reduce-scatter.7.cloned.1.call-start = ((), (), s32[]{:S(2)}) async-start(), calls=%async_computation.4 | async-start | bytes 5677056
  9.0 95.6 %copy-start.15 = (bf16[512,2,128]{2,1,0:T(2,128)(2,1)}, bf16[512,2,128]{2,1,0:T(2,128)(2,1)S(1)}, u32[]{:S(2)}) copy-start(bf16[512,2,128]{2,1,0:T(2,128)(2,1)S(1)} %reshape.322) | copy-start | bytes 786436
  9.9 94.8 %copy-start.25 = (f32[64]{0:T(128)}, f32[64]{0:T(128)S(1)}, u32[]{:S(2)}) copy-start(f32[64]{0:T(128)S(1)} %multiply_exponential_fusion) | copy-start | bytes 772
  11.8 92.9 %copy-start.26 = (f32[128]{0:T(128)S(1)}, f32[128]{0:T(128)}, u32[]{:S(2)}) copy-start(f32[128]{0:T(128)} %param.12) | copy-start | bytes 1540
  99.6 5.8 %copy-start.1 = (bf16[512,5376]{1,0:T(8,128)(2,1)S(1)}, bf16[512,5376]{1,0:T(8,128)(2,1)}, u32[]{:S(2)}) copy-start(bf16[512,5376]{1,0:T(8,128)(2,1)} %all-gather.2.cloned.1.call-done) | copy-start | bytes 16515076
  99.6 5.8 %copy-start.5 = (bf16[5376,128]{1,0:T(8,128)(2,1)S(1)}, bf16[5376,128]{1,0:T(8,128)(2,1)}, u32[]{:S(2)}) copy-start(bf16[5376,128]{1,0:T(8,128)(2,1)} %param.10) | copy-start | bytes 4128772
  105.4 3.4 copy-start.17
  107.4 0.7 copy-start.16
  108.7 12.0 %collective-permute-start.1 = (bf16[2,512,128]{1,2,0:T(8,128)(2,1)}, bf16[2,512,128]{1,2,0:T(8,128)(2,1)}, u32[]{:S(2)}, u32[]{:S(2)}) collective-permute-start(bf16[2,512,128]{1,2,0:T(8,128)(2,1)} %pad_maximum_fusion.1), channel_id=1, source_target_pairs={{0,8},{8,16},{16,24},{24,32},{32,40},{40,48},{48,56},{56,64},{64,7... | collective-permute-start | bytes 786440 | tf_op jit(solution)/shard_map/ppermute | solution.py:18
  110.7 12.3 %collective-permute-start = (bf16[2,512,128]{1,2,0:T(8,128)(2,1)}, bf16[2,512,128]{1,2,0:T(8,128)(2,1)}, u32[]{:S(2)}, u32[]{:S(2)}) collective-permute-start(bf16[2,512,128]{1,2,0:T(8,128)(2,1)} %pad_maximum_fusion.1), channel_id=1, source_target_pairs={{0,16},{8,24},{16,32},{24,40},{32,48},{40,56},{48,64},{56,72},{64,... | collective-permute-start | bytes 786440 | tf_op jit(solution)/shard_map/ppermute | solution.py:18
  117.6 6.6 %copy-start.4 = (pred[512,1536]{0,1:T(8,128)(4,1)S(1)}, pred[512,1536]{0,1:T(8,128)(4,1)}, u32[]{:S(2)}) copy-start(pred[512,1536]{0,1:T(8,128)(4,1)} %fusion.8) | copy-start | bytes 2359300
  120.7 3.5 copy-start.13
  124.2 2.5 copy-start.8
  125.4 4.2 copy-start.2
  126.7 2.9 copy-start.28
  126.7 2.9 copy-start.23
  138.9 5.5 %copy-start.9 = (bf16[2,1536,128]{1,2,0:T(8,128)(2,1)S(1)}, bf16[2,1536,128]{1,2,0:T(8,128)(2,1)}, u32[]{:S(2)}) copy-start(bf16[2,1536,128]{1,2,0:T(8,128)(2,1)} %copy-done.8) | copy-start | bytes 2359300
  138.9 7.2 %copy-start.14 = (bf16[512,2,128]{2,0,1:T(8,128)(2,1)S(1)}, bf16[512,2,128]{2,0,1:T(8,128)(2,1)}, u32[]{:S(2)}) copy-start(bf16[512,2,128]{2,0,1:T(8,128)(2,1)} %copy-done.13) | copy-start | bytes 786436
  144.4 2.9 copy-start.11
  144.4 2.9 copy-start.12
  144.4 3.7 copy-start.10
  146.0 8.7 %copy-start.27 = (f32[128]{0:T(128)S(1)}, f32[128]{0:T(128)}, u32[]{:S(2)}) copy-start(f32[128]{0:T(128)} %param.11) | copy-start | bytes 1540
  146.1 9.0 %copy-start.24 = (f32[512,2]{0,1:T(2,128)S(1)}, f32[512,2]{0,1:T(2,128)}, u32[]{:S(2)}) copy-start(f32[512,2]{0,1:T(2,128)} %get-tuple-element.89) | copy-start | bytes 12292
  147.3 0.9 copy-start.3
  149.2 12.3 %collective-permute-start.2 = (f32[2,512,128]{1,2,0:T(8,128)}, f32[2,512,128]{1,2,0:T(8,128)}, u32[]{:S(2)}, u32[]{:S(2)}) collective-permute-start(f32[2,512,128]{1,2,0:T(8,128)} %get-tuple-element.73), channel_id=1, source_target_pairs={{8,0},{16,8},{24,16},{32,24},{40,32},{48,40},{56,48},{64,56},{72,6... | collective-permute-start | bytes 1572872 | tf_op jit(solution)/shard_map/ppermute | solution.py:18
  151.3 21.4 %collective-permute-start.3 = (f32[2,512,128]{1,2,0:T(8,128)}, f32[2,512,128]{1,2,0:T(8,128)}, u32[]{:S(2)}, u32[]{:S(2)}) collective-permute-start(f32[2,512,128]{1,2,0:T(8,128)} %get-tuple-element.74), channel_id=1, source_target_pairs={{16,0},{24,8},{32,16},{40,24},{48,32},{56,40},{64,48},{72,56},{80,... | collective-permute-start | bytes 1572872 | tf_op jit(solution)/shard_map/ppermute | solution.py:18
  158.1 19.6 %copy-start.18 = (bf16[512,2,128]{0,2,1:T(8,128)(2,1)S(1)}, bf16[512,2,128]{0,2,1:T(8,128)(2,1)}, u32[]{:S(2)}) copy-start(bf16[512,2,128]{0,2,1:T(8,128)(2,1)} %copy.61) | copy-start | bytes 786436
  177.1 0.7 copy-start.20
  193.8 0.9 copy-start.19
  193.8 226.0 %reduce-scatter.5.cloned.1.call-start = ((), (), s32[]{:S(2)}) async-start(), calls=%async_computation.3 | async-start | bytes 6193152 | tf_op jit(solution)/shard_map/reduce_scatter | solution.py:216
  194.7 5.9 %copy-start.7 = (bf16[5376,128]{1,0:T(8,128)(2,1)S(1)}, bf16[5376,128]{1,0:T(8,128)(2,1)}, u32[]{:S(2)}) copy-start(bf16[5376,128]{1,0:T(8,128)(2,1)} %param.9) | copy-start | bytes 4128772
  194.7 5.9 %copy-start.21 = (bf16[512,128]{0,1:T(8,128)(2,1)S(1)}, bf16[512,128]{0,1:T(8,128)(2,1)}, u32[]{:S(2)}) copy-start(bf16[512,128]{0,1:T(8,128)(2,1)} %copy-done.20) | copy-start | bytes 393220
  200.6 5.7 %copy-start.6 = (bf16[5376,128]{1,0:T(8,128)(2,1)S(1)}, bf16[5376,128]{1,0:T(8,128)(2,1)}, u32[]{:S(2)}) copy-start(bf16[5376,128]{1,0:T(8,128)(2,1)} %param.10) | copy-start | bytes 4128772
  217.7 1.0 copy-start.22
Sparse Core Ops, SparseCore 0:
  10.6 88.9 all-gather.1
  193.9 118.0 reduce-scatter.6
  316.7 103.0 reduce-scatter.4
where the time goes:
time: 428 us; the launch traced here: 426 us
  waiting for transfers between devices  300 us (70%)
  matrix products  56.2 us (13%)
  local copies, waits for them, and re-layouts  25 us (6%)
  other arithmetic  20.3 us (5%)
  between operations  14.3 us (3%)
  starting transfers between devices  10.2 us (2%)
    reduce_scatter x1, waiting for transfers between devices, per_device(): lax.psum_scatter((partial_sum + lax.dot_general(grad_value, value_weight,...  104 us
    unnamed x4, waiting for transfers between devices  93.2 us
    all_gather x1, waiting for transfers between devices, per_device(): gathered = lax.all_gather(hidden, 'heads', axis=0, tiled=True)  85.8 us
    unnamed x65, local copies, waits for them, and re-layouts  18.3 us
    ppermute x4, waiting for transfers between devices, passed_along(): return lax.ppermute(block, axis, route)  16.9 us
    dot_general x1, matrix products, per_device(): lax.dot_general(grad_value, value_weight, back_contract, preferred_elemen...  11.4 us
    ppermute x4, starting transfers between devices, passed_along(): return lax.ppermute(block, axis, route)  10 us
  transfers between devices with their start and end apart: 7, of which 6 were waited for; matrix products, arithmetic and copies ran while one was open for 10% of the time, Pallas kernels for 0%

commit v1 on v0

--- a/solution.py
+++ b/solution.py
@@ -16,6 +16,42 @@
     devices = range(lax.axis_size(axis))
     route = [(i - distance, i) for i in devices if i - distance in devices]
     return lax.ppermute(block, axis, route)
+
+
+def torus_shifts(axis):
+    size = lax.axis_size(axis)
+    inner = size // 2 if size >= 4 else size
+    outer = size // inner
+    me = lax.axis_index(axis)
+
+    def moved(index, dx, dy):
+        return ((index // inner + dx) % outer) * inner + (index % inner + dy) % inner
+
+    shifts = [(dx, dy) for dx in range(outer) for dy in range(inner)][1:]
+    routes = [[(i, moved(i, dx, dy)) for i in range(size)] for dx, dy in shifts]
+    targets = [moved(me, dx, dy) for dx, dy in shifts]
+    slot_of = [
+        ((me // inner - j // inner) % outer) * inner + (me % inner - j % inner) % inner
+        for j in range(size)
+    ]
+    return (size, me, routes, targets, slot_of)
+
+
+def gather_over(block, axis):
+    size, me, routes, targets, slot_of = torus_shifts(axis)
+    slots = jnp.stack([block] + [lax.ppermute(block, axis, route) for route in routes])
+    order = jnp.stack([jnp.asarray(s, jnp.int32) for s in slot_of])
+    return jnp.take(slots, order, axis=0).reshape((size * block.shape[0],) + block.shape[1:])
+
+
+def scatter_sum_over(full, axis):
+    size, me, routes, targets, slot_of = torus_shifts(axis)
+    pieces = full.reshape((size, full.shape[0] // size) + full.shape[1:])
+    total = lax.dynamic_index_in_dim(pieces, me, 0, keepdims=False).astype(jnp.float32)
+    for route, target in zip(routes, targets):
+        piece = lax.dynamic_index_in_dim(pieces, target, 0, keepdims=False)
+        total = total + lax.ppermute(piece, axis, route).astype(jnp.float32)
+    return total
 
 
 def rope_tables(positions, head_size):
@@ -121,7 +157,7 @@
     window_rows = block_rows + WINDOW
     reach_blocks = (WINDOW - 2) // token_count + 1
     position_base = lax.axis_index("ctx") * token_count
-    gathered = lax.all_gather(hidden, "heads", axis=0, tiled=True)
+    gathered = gather_over(hidden, "heads")
     query_proj = jnp.dot(gathered, query_weight, preferred_element_type=jnp.float32)
     key_proj = jnp.dot(gathered, key_weight, preferred_element_type=jnp.float32)
     value_proj = jnp.dot(gathered, value_weight, preferred_element_type=jnp.float32)
@@ -213,7 +249,7 @@
     partial_sum = partial_sum + lax.dot_general(
         grad_key, key_weight, back_contract, preferred_element_type=jnp.float32
     )
-    input_grad = lax.psum_scatter(
+    input_grad = scatter_sum_over(
         (
             partial_sum
             + lax.dot_general(
@@ -221,9 +257,7 @@
             )
         ).astype(jnp.bfloat16),
         "heads",
-        scatter_dimension=0,
-        tiled=True,
-    )
+    ).astype(jnp.bfloat16)
     return (attention, input_grad, query_weight_grad, key_weight_grad, value_weight_grad)
 
 

time: 428 us -> 331 us (0.77)
  waiting for transfers between devices: 300 us -> 133 us
  starting transfers between devices: 10.2 us -> 71 us
  local copies, waits for them, and re-layouts: 25 us -> 37.5 us
    ppermute x0 -> x14, waiting for transfers between devices: none -> 115 us  [the longest x7 107 us: scatter_sum_over(): total = total + lax.ppermute(piece, axis, route).astype(jnp.float32)]
    reduce_scatter x1, waiting for transfers between devices: 104 us -> 0.01 us  [per_device(): lax.psum_scatter((lax.dot_general(gathered, jnp.concatenate([grad_query,...]
    unnamed x4 -> x1, waiting for transfers between devices: 93.2 us -> 0.02 us
    all_gather x1 -> x0, waiting for transfers between devices: 85.8 us -> none  [per_device(): gathered = lax.all_gather(hidden, 'heads', axis=0, tiled=True)]
    ppermute x0 -> x14, starting transfers between devices: none -> 60.7 us  [the longest x7 47.2 us: gather_over(): lax.ppermute(block, axis, route)]
    dot_general x1, matrix products: 1.63 us -> 10.7 us  [attend_backward(): jnp.einsum('kgqj,jkd->qkgd', shifts, key_grid, preferred_element_type=jnp...]
    gather x0 -> x1, local copies, waits for them, and re-layouts: none -> 5.92 us  [gather_over(): jnp.take(slots, order, axis=0)]
    dot_general x0 -> x1, local copies, waits for them, and re-layouts: none -> 4.53 us  [per_device(): jnp.dot(gathered, query_weight, preferred_element_type=jnp.float32)]
  transfers between devices with their start and end apart: 7 -> 19, of which waited for: 6 -> 12; matrix products, arithmetic and copies ran while one was open for 10% -> 16% of each run, Pallas kernels for 0% -> 0%
where the time goes in v1:
time: 331 us; the launch traced here: 327 us
  waiting for transfers between devices  133 us (40%)
  starting transfers between devices  71 us (21%)
  matrix products  52.6 us (16%)
  local copies, waits for them, and re-layouts  37.5 us (11%)
  other arithmetic  17.7 us (5%)
  between operations  15 us (5%)
    ppermute x7, waiting for transfers between devices, scatter_sum_over(): total = total + lax.ppermute(piece, axis, route).astype(jnp.float32)  107 us
    ppermute x7, starting transfers between devices, gather_over(): lax.ppermute(block, axis, route)  47.2 us
    ppermute x4, waiting for transfers between devices, passed_along(): return lax.ppermute(block, axis, route)  18 us
    unnamed x63, local copies, waits for them, and re-layouts  15.9 us
    ppermute x7, starting transfers between devices, scatter_sum_over(): total = total + lax.ppermute(piece, axis, route).astype(jnp.float32)  13.5 us
    dot_general x1, matrix products, attend_backward(): jnp.einsum('kgqj,jkd->qkgd', shifts, key_grid, preferred_element_type=jnp...  10.7 us
    ppermute x4, starting transfers between devices, passed_along(): return lax.ppermute(block, axis, route)  10.2 us
    dot_general x1, matrix products, per_device(): lax.dot_general(grad_value, value_weight, back_contract, preferred_elemen...  8.58 us
  transfers between devices with their start and end apart: 19, of which 12 were waited for; matrix products, arithmetic and copies ran while one was open for 16% of the time, Pallas kernels for 0%

profile of v1, /device:TPU:96, one launch (start us, length us, event | category | flops | bytes accessed | tf_op | source)
XLA Modules:
  0.0 326.8 jit_solution(13044986777557538298)
XLA Ops:
  7.2 1.7 collective-permute-start
  8.9 2.9 collective-permute-start.1
  11.8 1.3 collective-permute-start.2
  13.1 3.0 collective-permute-start.3
  16.2 0.6 collective-permute-start.4
  16.8 2.0 bitcast_dynamic-update-slice_fusion.7
  19.6 0.6 pad_clamp_fusion
  20.4 0.6 broadcast_in_dim.84
  21.0 4.5 %copy.40 = bf16[256,5376]{1,0:T(8,128)(2,1)} copy(bf16[256,5376]{0,1:T(8,128)(2,1)} %bitcast.196) | data formatting | bytes 5505024 | tf_op jit(solution)/shard_map/dot_general | solution.py:161
  25.6 0.9 copy.22
  26.5 1.2 multiply_cosine_fusion
  27.7 1.9 fusion.7
  29.7 37.7 %collective-permute-start.5 = (bf16[64,5376]{1,0:T(8,128)(2,1)S(1)}, bf16[64,5376]{1,0:T(8,128)(2,1)S(1)}, u32[]{:S(2)}, u32[]{:S(2)}) collective-permute-start(bf16[64,5376]{1,0:T(8,128)(2,1)S(1)} %copy-done.13), channel_id=1, source_target_pairs={{0,6},{1,7},{2,4},{3,5},{4,2},{5,3},{6,0},{7,1},{8,14},{9,15},{10,... | collective-permute-start | bytes 2064392 | tf_op jit(solution)/shard_map/ppermute | solution.py:42
  67.3 2.0 bitcast_dynamic-update-slice_fusion.6
  69.4 2.0 bitcast_dynamic-update-slice_fusion.5
  71.4 2.0 bitcast_dynamic-update-slice_fusion.4
  73.4 2.0 bitcast_dynamic-update-slice_fusion.3
  75.4 0.9 bitcast_dynamic-update-slice_fusion.2
  76.3 5.5 %collective-permute-done.5 = bf16[64,5376]{1,0:T(8,128)(2,1)S(1)} collective-permute-done((bf16[64,5376]{1,0:T(8,128)(2,1)S(1)}, bf16[64,5376]{1,0:T(8,128)(2,1)S(1)}, u32[]{:S(2)}, u32[]{:S(2)}) %collective-permute-start.5) | collective-permute-done | bytes 688160 | tf_op jit(solution)/shard_map/ppermute | solution.py:42
  81.8 0.9 bitcast_dynamic-update-slice_fusion.1
  82.8 2.9 collective-permute-done.6
  85.6 0.9 bitcast_dynamic-update-slice_fusion
  86.6 5.9 %gather_fusion = bf16[8,64,5376]{2,1,0:T(8,128)(2,1)} fusion(bf16[8,64,5376]{2,1,0:T(8,128)(2,1)} %bitcast_dynamic-update-slice_fusion, s32[1024]{0:T(1024)} %pad_clamp_fusion), kind=kCustom, calls=%fused_computation | custom fusion | bytes 11010080 | tf_op jit(solution)/shard_map/jit(_take)/gather | solution.py:44
  92.5 3.1 bitcast_select_fusion.1
  95.7 2.0 multiply_reduce_fusion.3
  98.4 1.9 fusion.16
  100.4 3.7 %collective-permute-start.7 = (bf16[2,512,128]{1,2,0:T(8,128)(2,1)S(1)}, bf16[2,512,128]{1,2,0:T(8,128)(2,1)S(1)}, u32[]{:S(2)}, u32[]{:S(2)}) collective-permute-start(bf16[2,512,128]{1,2,0:T(8,128)(2,1)S(1)} %pad_maximum_fusion.1), channel_id=1, source_target_pairs={{0,16},{8,24},{16,32},{24,40},{32,48},{40,56},{48,64},{56,72},{64,... | collective-permute-start | bytes 786440 | tf_op jit(solution)/shard_map/ppermute | solution.py:18
  104.1 2.2 collective-permute-start.8
  106.9 1.6 multiply_reduce_fusion.2
  108.8 1.0 collective-permute-done.7
  109.8 2.8 collective-permute-done.8
  112.7 1.3 fusion.2
  114.0 1.3 exponential_reduce_fusion
  115.3 2.9 bitcast_convert_fusion
  118.2 3.0 convolution_bitcast_fusion
  121.2 2.0 copy.34
  123.3 2.4 multiply_reduce_fusion
  125.7 1.1 copy.35
  126.8 5.3 %fusion.4 = bf16[2,512,1536]{1,2,0:T(8,128)(2,1)S(1)} fusion(bf16[512,2,128]{0,2,1:T(8,128)(2,1)} %copy.22, f32[1536,512,2]{1,0,2:T(8,128)} %copy-done.2, f32[2,512]{1,0:T(2,128)S(1)} %copy.35, f32[2,512]{1,0:T(2,128)S(1)} %log_add_fusion, pred[512,1536]{0,1:T(8,128)(4,1)S(1)} %fusion.7, bf16[2,1536,128]{1,2,0:T(8,128)(2,1)} %copy-done.4), kind=kOutput, calls=%fused_computation.15 | convolution fusion | flops 412090368 | bytes 10887168 | tf_op jit(solution)/shard_map/while/body/eval_jaxpr/qkgd,jkd->kgqj/dot_general | solution.py:133
  132.2 1.2 convolution_bitcast_fusion.1
  133.3 10.7 %fusion.15 = f32[512,2,128]{0,2,1:T(8,128)S(1)} fusion(bf16[2,512,1536]{1,2,0:T(8,128)(2,1)S(1)} %fusion.4, bf16[2,1536,128]{1,2,0:T(8,128)(2,1)S(1)} %copy-done.5), kind=kOutput, calls=%fused_computation.34 | convolution fusion | flops 402784256 | bytes 4063232 | tf_op jit(solution)/shard_map/while/body/eval_jaxpr/kgqj,jkd->qkgd/dot_general | solution.py:137
  144.2 2.4 collective-permute-start.10
  146.6 1.9 collective-permute-start.9
  149.0 10.7 %collective-permute-done.10 = f32[2,512,128]{1,2,0:T(8,128)S(1)} collective-permute-done((f32[2,512,128]{1,2,0:T(8,128)S(1)}, f32[2,512,128]{1,2,0:T(8,128)S(1)}, u32[]{:S(2)}, u32[]{:S(2)}) %collective-permute-start.10) | collective-permute-done | bytes 524320 | tf_op jit(solution)/shard_map/ppermute | solution.py:18
  159.7 3.4 %collective-permute-done.9 = f32[2,512,128]{1,2,0:T(8,128)S(1)} collective-permute-done((f32[2,512,128]{1,2,0:T(8,128)S(1)}, f32[2,512,128]{1,2,0:T(8,128)S(1)}, u32[]{:S(2)}, u32[]{:S(2)}) %collective-permute-start.9) | collective-permute-done | bytes 524320 | tf_op jit(solution)/shard_map/ppermute | solution.py:18
  164.2 4.9 %multiply_convert_fusion = bf16[5376,512]{1,0:T(8,128)(2,1)} fusion(bf16[512,5376]{1,0:T(8,128)(2,1)S(1)} %bitcast.191, bf16[512,128]{0,1:T(8,128)(2,1)S(1)} %fusion.45, bf16[512,128]{0,1:T(8,128)(2,1)S(1)} %fusion.46, bf16[512,256]{0,1:T(8,128)(2,1)S(1)} %bitcast.199), kind=kOutput, calls=%fused_computation.1 | convolution fusion | flops 2825650176 | bytes 11534336 | tf_op jit(solution)/shard_map/dot_general | solution.py:230
  169.3 7.6 %fusion.62 = f32[512,5376]{1,0:T(8,128)} fusion(bf16[512,256]{0,1:T(8,128)(2,1)S(1)} %bitcast.200, bf16[5376,256]{1,0:T(8,128)(2,1)} %param.8), kind=kOutput, calls=%fused_computation.135 | convolution fusion | flops 1409286144 | bytes 14024704 | tf_op jit(solution)/shard_map/dot_general | solution.py:246
  176.9 1.6 fusion.63
  178.5 8.6 %add_convert_fusion = bf16[512,5376]{1,0:T(8,128)(2,1)} fusion(f32[512,5376]{1,0:T(8,128)} %fusion.62, f32[512,5376]{1,0:T(8,128)S(1)} %fusion.63, bf16[5376,128]{1,0:T(8,128)(2,1)} %param.10, f32[2,512,128]{1,2,0:T(8,128)S(1)} %fusion.21), kind=kOutput, calls=%fused_computation.2 | convolution fusion | flops 712900608 | bytes 29032448 | tf_op jit(solution)/shard_map/dot_general | solution.py:255
  187.1 4.2 %dynamic-slice_bitcast_fusion.6 = (bf16[64,5376]{1,0:T(8,128)(2,1)S(1)}, bf16[64,5376]{1,0:T(8,128)(2,1)}, bf16[64,5376]{1,0:T(8,128)(2,1)}, bf16[64,5376]{1,0:T...) fusion(bf16[8,64,5376]{2,1,0:T(8,128)(2,1)} %bitcast.194, ...), kind=kLoop, calls=%fused_computation.54 | loop fusion | bytes 9633820 | tf_op jit(solution)/shard_map/jit(dynamic_index_in_dim)/squeeze | solution.py:52
  191.3 3.5 %collective-permute-start.11 = (bf16[64,5376]{1,0:T(8,128)(2,1)S(1)}, bf16[64,5376]{1,0:T(8,128)(2,1)S(1)}, u32[]{:S(2)}, u32[]{:S(2)}) collective-permute-start(bf16[64,5376]{1,0:T(8,128)(2,1)S(1)} %get-tuple-element.52), channel_id=1, source_target_pairs={{0,1},{1,2},{2,3},{3,0},{4,5},{5,6},{6,7},{7,4},{8,9},{9,10},{10,1... | collective-permute-start | bytes 2064392 | tf_op jit(solution)/shard_map/ppermute | solution.py:53
  194.8 4.3 %collective-permute-start.12 = (bf16[64,5376]{1,0:T(8,128)(2,1)S(1)}, bf16[64,5376]{1,0:T(8,128)(2,1)S(1)}, u32[]{:S(2)}, u32[]{:S(2)}) collective-permute-start(bf16[64,5376]{1,0:T(8,128)(2,1)S(1)} %get-tuple-element.58), channel_id=1, source_target_pairs={{0,2},{1,3},{2,0},{3,1},{4,6},{5,7},{6,4},{7,5},{8,10},{9,11},{10,... | collective-permute-start | bytes 2064392 | tf_op jit(solution)/shard_map/ppermute | solution.py:53
  199.5 4.5 %collective-permute-start.15 = (bf16[64,5376]{1,0:T(8,128)(2,1)}, bf16[64,5376]{1,0:T(8,128)(2,1)}, u32[]{:S(2)}, u32[]{:S(2)}) collective-permute-start(bf16[64,5376]{1,0:T(8,128)(2,1)} %get-tuple-element.55), channel_id=1, source_target_pairs={{0,5},{1,6},{2,7},{3,4},{4,1},{5,2},{6,3},{7,0},{8,13},{9,14},{10,... | collective-permute-start | bytes 2064392 | tf_op jit(solution)/shard_map/ppermute | solution.py:53
  204.1 8.6 %collective-permute-done.11 = bf16[64,5376]{1,0:T(8,128)(2,1)S(1)} collective-permute-done((bf16[64,5376]{1,0:T(8,128)(2,1)S(1)}, bf16[64,5376]{1,0:T(8,128)(2,1)S(1)}, u32[]{:S(2)}, u32[]{:S(2)}) %collective-permute-start.11) | collective-permute-done | bytes 688160 | tf_op jit(solution)/shard_map/ppermute | solution.py:53
  212.6 0.8 collective-permute-start.16
  213.4 15.7 %collective-permute-done.12 = bf16[64,5376]{1,0:T(8,128)(2,1)S(1)} collective-permute-done((bf16[64,5376]{1,0:T(8,128)(2,1)S(1)}, bf16[64,5376]{1,0:T(8,128)(2,1)S(1)}, u32[]{:S(2)}, u32[]{:S(2)}) %collective-permute-start.12) | collective-permute-done | bytes 688160 | tf_op jit(solution)/shard_map/ppermute | solution.py:53
  229.1 1.8 copy.23
  230.9 2.2 collective-permute-done.14
  233.1 26.0 %collective-permute-done.15 = bf16[64,5376]{1,0:T(8,128)(2,1)} collective-permute-done((bf16[64,5376]{1,0:T(8,128)(2,1)}, bf16[64,5376]{1,0:T(8,128)(2,1)}, u32[]{:S(2)}, u32[]{:S(2)}) %collective-permute-start.15) | collective-permute-done | bytes 688160 | tf_op jit(solution)/shard_map/ppermute | solution.py:53
  259.1 30.0 %collective-permute-done.16 = bf16[64,5376]{1,0:T(8,128)(2,1)} collective-permute-done((bf16[64,5376]{1,0:T(8,128)(2,1)}, bf16[64,5376]{1,0:T(8,128)(2,1)}, u32[]{:S(2)}, u32[]{:S(2)}) %collective-permute-start.16) | collective-permute-done | bytes 688160 | tf_op jit(solution)/shard_map/ppermute | solution.py:53
  289.2 24.1 %collective-permute-done.17 = bf16[64,5376]{1,0:T(8,128)(2,1)} collective-permute-done((bf16[64,5376]{1,0:T(8,128)(2,1)}, bf16[64,5376]{1,0:T(8,128)(2,1)}, u32[]{:S(2)}, u32[]{:S(2)}) %collective-permute-start.17) | collective-permute-done | bytes 688160 | tf_op jit(solution)/shard_map/ppermute | solution.py:53
  313.3 3.5 %fusion.14 = bf16[64,5376]{1,0:T(8,128)(2,1)} fusion(bf16[64,5376]{1,0:T(8,128)(2,1)} %collective-permute-done.17, bf16[64,5376]{1,0:T(8,128)(2,1)} %collective-permute-done.16, bf16[64,5376]{1,0:T(8,128)(2,1)} %collective-permute-done.15, bf16[64,5376]{1,0:T(8,128)(2,1)} %collective-permute-done.14, bf16[64,5376]{1,0:T(8,128)(2,1)S(1)} %collective-permute-done.13, ...), kind=kLoop, calls=%fused_computation.32 | loop fusion | flops 5505024 | bytes 6193156 | tf_op jit(solution)/shard_map/convert_element_type | solution.py:260
  316.7 1.5 fusion.60
  318.2 1.6 slice.71
  (103 shorter events, 4.7 us)
Async XLA Ops:
  7.2 88.4 %copy-start = (bf16[5376,128]{1,0:T(8,128)(2,1)S(1)}, bf16[5376,128]{1,0:T(8,128)(2,1)}, u32[]{:S(2)}) copy-start(bf16[5376,128]{1,0:T(8,128)(2,1)} %param.9) | copy-start | bytes 4128772
  7.2 22.5 %copy-start.13 = (bf16[64,5376]{1,0:T(8,128)(2,1)S(1)}, bf16[64,5376]{1,0:T(8,128)(2,1)}, u32[]{:S(2)}) copy-start(bf16[64,5376]{1,0:T(8,128)(2,1)} %param.7) | copy-start | bytes 2064388
  7.2 18.4 %copy-start.14 = (bf16[512,256]{1,0:T(8,128)(2,1)S(1)}, bf16[512,256]{1,0:T(8,128)(2,1)}, u32[]{:S(2)}) copy-start(bf16[512,256]{1,0:T(8,128)(2,1)} %param.13) | copy-start | bytes 786436
  7.2 309.5 %reduce-scatter.2.cloned.1.call-start = ((), (), s32[]{:S(2)}) async-start(), calls=%async_computation.1 | async-start | bytes 5677056 | tf_op jit(solution)/shard_map/reduce_scatter | solution.py:228
  7.2 22.4 %collective-permute-start = (bf16[64,5376]{1,0:T(8,128)(2,1)}, bf16[64,5376]{1,0:T(8,128)(2,1)}, u32[]{:S(2)}, u32[]{:S(2)}) collective-permute-start(bf16[64,5376]{1,0:T(8,128)(2,1)} %param.7), channel_id=1, source_target_pairs={{0,1},{1,2},{2,3},{3,0},{4,5},{5,6},{6,7},{7,4},{8,9},{9,10},{10,1... | collective-permute-start | bytes 2064392 | tf_op jit(solution)/shard_map/ppermute | solution.py:42
  8.9 60.5 %collective-permute-start.1 = (bf16[64,5376]{1,0:T(8,128)(2,1)}, bf16[64,5376]{1,0:T(8,128)(2,1)}, u32[]{:S(2)}, u32[]{:S(2)}) collective-permute-start(bf16[64,5376]{1,0:T(8,128)(2,1)} %param.7), channel_id=1, source_target_pairs={{0,2},{1,3},{2,0},{3,1},{4,6},{5,7},{6,4},{7,5},{8,10},{9,11},{10,... | collective-permute-start | bytes 2064392 | tf_op jit(solution)/shard_map/ppermute | solution.py:42
  11.8 59.6 %collective-permute-start.2 = (bf16[64,5376]{1,0:T(8,128)(2,1)}, bf16[64,5376]{1,0:T(8,128)(2,1)}, u32[]{:S(2)}, u32[]{:S(2)}) collective-permute-start(bf16[64,5376]{1,0:T(8,128)(2,1)} %param.7), channel_id=1, source_target_pairs={{0,3},{1,0},{2,1},{3,2},{4,7},{5,4},{6,5},{7,6},{8,11},{9,8},{10,9... | collective-permute-start | bytes 2064392 | tf_op jit(solution)/shard_map/ppermute | solution.py:42
  13.1 60.2 %collective-permute-start.3 = (bf16[64,5376]{1,0:T(8,128)(2,1)}, bf16[64,5376]{1,0:T(8,128)(2,1)}, u32[]{:S(2)}, u32[]{:S(2)}) collective-permute-start(bf16[64,5376]{1,0:T(8,128)(2,1)} %param.7), channel_id=1, source_target_pairs={{0,4},{1,5},{2,6},{3,7},{4,0},{5,1},{6,2},{7,3},{8,12},{9,13},{10,... | collective-permute-start | bytes 2064392 | tf_op jit(solution)/shard_map/ppermute | solution.py:42
  16.2 59.2 %collective-permute-start.4 = (bf16[64,5376]{1,0:T(8,128)(2,1)}, bf16[64,5376]{1,0:T(8,128)(2,1)S(1)}, u32[]{:S(2)}, u32[]{:S(2)}) collective-permute-start(bf16[64,5376]{1,0:T(8,128)(2,1)} %param.7), channel_id=1, source_target_pairs={{0,5},{1,6},{2,7},{3,4},{4,1},{5,2},{6,3},{7,0},{8,13},{9,14},{10,... | collective-permute-start | bytes 2064392 | tf_op jit(solution)/shard_map/ppermute | solution.py:42
  18.9 7.7 %copy-start.17 = (f32[64]{0:T(128)}, f32[64]{0:T(128)S(1)}, u32[]{:S(2)}) copy-start(f32[64]{0:T(128)S(1)} %multiply_exponential_fusion) | copy-start | bytes 772
  20.3 6.2 %copy-start.20 = (pred[8]{0:T(512)(128)(4,1)}, pred[8]{0:T(512)(128)(4,1)S(1)}, u32[]{:S(2)}) copy-start(pred[8]{0:T(512)(128)(4,1)S(1)} %compare_and_fusion) | copy-start | bytes 28
  25.6 0.9 copy-start.8
  29.7 52.2 %collective-permute-start.5 = (bf16[64,5376]{1,0:T(8,128)(2,1)S(1)}, bf16[64,5376]{1,0:T(8,128)(2,1)S(1)}, u32[]{:S(2)}, u32[]{:S(2)}) collective-permute-start(bf16[64,5376]{1,0:T(8,128)(2,1)S(1)} %copy-done.13), channel_id=1, source_target_pairs={{0,6},{1,7},{2,4},{3,5},{4,2},{5,3},{6,0},{7,1},{8,14},{9,15},{10,... | collective-permute-start | bytes 2064392 | tf_op jit(solution)/shard_map/ppermute | solution.py:42
  69.4 16.3 %collective-permute-start.6 = (bf16[64,5376]{1,0:T(8,128)(2,1)S(1)}, bf16[64,5376]{1,0:T(8,128)(2,1)S(1)}, u32[]{:S(2)}, u32[]{:S(2)}) collective-permute-start(bf16[64,5376]{1,0:T(8,128)(2,1)S(1)} %copy-done.13), channel_id=1, source_target_pairs={{0,7},{1,4},{2,5},{3,6},{4,3},{5,0},{6,1},{7,2},{8,15},{9,12},{10,... | collective-permute-start | bytes 2064392 | tf_op jit(solution)/shard_map/ppermute | solution.py:42
  86.6 5.9 %copy-start.22 = (pred[512]{0:T(512)(128)(4,1)S(1)}, pred[512]{0:T(512)(128)(4,1)}, u32[]{:S(2)}) copy-start(pred[512]{0:T(512)(128)(4,1)} %broadcast_in_dim.84) | copy-start | bytes 1540
  95.6 4.7 %copy-start.1 = (bf16[512,5376]{1,0:T(8,128)(2,1)}, bf16[512,5376]{1,0:T(8,128)(2,1)S(1)}, u32[]{:S(2)}) copy-start(bf16[512,5376]{1,0:T(8,128)(2,1)S(1)} %bitcast_select_fusion.1) | copy-start | bytes 16515076
  95.6 2.0 copy-start.19
  95.6 2.1 copy-start.18
  95.6 2.7 copy-start.3
  97.8 8.5 %slice-start.2 = ((s8[5505024]{0:T(1024)(128)(4,1)}), s8[4194304]{0:T(1024)(128)(4,1)S(1)}, s32[]{:S(2)}) async-start(s8[5505024]{0:T(1024)(128)(4,1)} %bitcast.192), calls=%async_computation.4 | async-start | bytes 8388608
  97.8 8.5 %copy-start.21 = (pred[8]{0:T(512)(128)(4,1)S(1)}, pred[8]{0:T(512)(128)(4,1)}, u32[]{:S(2)}) copy-start(pred[8]{0:T(512)(128)(4,1)} %copy-done.20) | copy-start | bytes 28
  98.4 7.9 %slice-start.3 = ((s8[5505024]{0:T(1024)(128)(4,1)}), s8[1310720]{0:T(1024)(128)(4,1)S(1)}, s32[]{:S(2)}) async-start(s8[5505024]{0:T(1024)(128)(4,1)} %bitcast.192), calls=%async_computation.5 | async-start | bytes 2621440
  100.4 6.5 %copy-start.7 = (bf16[256,5376]{1,0:T(8,128)(2,1)S(1)}, bf16[256,5376]{1,0:T(8,128)(2,1)}, u32[]{:S(2)}) copy-start(bf16[256,5376]{1,0:T(8,128)(2,1)} %copy.40) | copy-start | bytes 8257540
  100.4 9.4 %collective-permute-start.7 = (bf16[2,512,128]{1,2,0:T(8,128)(2,1)S(1)}, bf16[2,512,128]{1,2,0:T(8,128)(2,1)S(1)}, u32[]{:S(2)}, u32[]{:S(2)}) collective-permute-start(bf16[2,512,128]{1,2,0:T(8,128)(2,1)S(1)} %pad_maximum_fusion.1), channel_id=1, source_target_pairs={{0,16},{8,24},{16,32},{24,40},{32,48},{40,56},{48,64},{56,72},{64,... | collective-permute-start | bytes 786440 | tf_op jit(solution)/shard_map/ppermute | solution.py:18
  104.1 8.6 %collective-permute-start.8 = (bf16[2,512,128]{1,2,0:T(8,128)(2,1)S(1)}, bf16[2,512,128]{1,2,0:T(8,128)(2,1)S(1)}, u32[]{:S(2)}, u32[]{:S(2)}) collective-permute-start(bf16[2,512,128]{1,2,0:T(8,128)(2,1)S(1)} %pad_maximum_fusion.1), channel_id=1, source_target_pairs={{0,8},{8,16},{16,24},{24,32},{32,40},{40,48},{48,56},{56,64},{64,7... | collective-permute-start | bytes 786440 | tf_op jit(solution)/shard_map/ppermute | solution.py:18
  106.9 1.7 copy-start.16
  106.9 1.8 copy-start.9
  106.9 1.8 copy-start.11
  112.7 2.6 copy-start.4
  114.0 4.2 %copy-start.2 = (f32[1536,512,2]{1,0,2:T(8,128)}, f32[1536,512,2]{1,0,2:T(8,128)S(1)}, u32[]{:S(2)}) copy-start(f32[1536,512,2]{1,0,2:T(8,128)S(1)} %get-tuple-element.89) | copy-start | bytes 18874372
  115.3 2.9 copy-start.15
  126.8 6.5 %copy-start.5 = (bf16[2,1536,128]{1,2,0:T(8,128)(2,1)S(1)}, bf16[2,1536,128]{1,2,0:T(8,128)(2,1)}, u32[]{:S(2)}) copy-start(bf16[2,1536,128]{1,2,0:T(8,128)(2,1)} %copy-done.4) | copy-start | bytes 2359300
  132.1 11.9 %copy-start.6 = (f32[1,1536,128]{1,2,0:T(8,128)S(1)}, f32[1,1536,128]{1,2,0:T(8,128)}, u32[]{:S(2)}) copy-start(f32[1,1536,128]{1,2,0:T(8,128)} %convolution_bitcast_fusion) | copy-start | bytes 2359300
  132.1 16.4 %copy-start.10 = (f32[512,64]{0,1:T(8,128)S(1)}, f32[512,64]{0,1:T(8,128)}, u32[]{:S(2)}) copy-start(f32[512,64]{0,1:T(8,128)} %get-tuple-element.82) | copy-start | bytes 393220
  132.1 16.4 %copy-start.12 = (f32[512,64]{0,1:T(8,128)S(1)}, f32[512,64]{0,1:T(8,128)}, u32[]{:S(2)}) copy-start(f32[512,64]{0,1:T(8,128)} %get-tuple-element.83) | copy-start | bytes 393220
  133.3 30.9 %slice-start = ((s8[5505024]{0:T(1024)(128)(4,1)}), s8[4194304]{0:T(1024)(128)(4,1)S(1)}, s32[]{:S(2)}) async-start(s8[5505024]{0:T(1024)(128)(4,1)} %bitcast.190), calls=%async_computation.2 | async-start | bytes 8388608
  144.2 15.6 %collective-permute-start.10 = (f32[2,512,128]{1,2,0:T(8,128)S(1)}, f32[2,512,128]{1,2,0:T(8,128)S(1)}, u32[]{:S(2)}, u32[]{:S(2)}) collective-permute-start(f32[2,512,128]{1,2,0:T(8,128)S(1)} %get-tuple-element.60), channel_id=1, source_target_pairs={{16,0},{24,8},{32,16},{40,24},{48,32},{56,40},{64,48},{72,56},{80,... | collective-permute-start | bytes 1572872 | tf_op jit(solution)/shard_map/ppermute | solution.py:18
  146.6 16.5 %collective-permute-start.9 = (f32[2,512,128]{1,2,0:T(8,128)S(1)}, f32[2,512,128]{1,2,0:T(8,128)S(1)}, u32[]{:S(2)}, u32[]{:S(2)}) collective-permute-start(f32[2,512,128]{1,2,0:T(8,128)S(1)} %get-tuple-element.59), channel_id=1, source_target_pairs={{8,0},{16,8},{24,16},{32,24},{40,32},{48,40},{56,48},{64,56},{72,6... | collective-permute-start | bytes 1572872 | tf_op jit(solution)/shard_map/ppermute | solution.py:18
  148.7 15.6 %slice-start.1 = ((s8[5505024]{0:T(1024)(128)(4,1)}), s8[1310720]{0:T(1024)(128)(4,1)S(1)}, s32[]{:S(2)}) async-start(s8[5505024]{0:T(1024)(128)(4,1)} %bitcast.190), calls=%async_computation.3 | async-start | bytes 2621440
  191.3 21.3 %collective-permute-start.11 = (bf16[64,5376]{1,0:T(8,128)(2,1)S(1)}, bf16[64,5376]{1,0:T(8,128)(2,1)S(1)}, u32[]{:S(2)}, u32[]{:S(2)}) collective-permute-start(bf16[64,5376]{1,0:T(8,128)(2,1)S(1)} %get-tuple-element.52), channel_id=1, source_target_pairs={{0,1},{1,2},{2,3},{3,0},{4,5},{5,6},{6,7},{7,4},{8,9},{9,10},{10,1... | collective-permute-start | bytes 2064392 | tf_op jit(solution)/shard_map/ppermute | solution.py:53
  194.8 34.3 %collective-permute-start.12 = (bf16[64,5376]{1,0:T(8,128)(2,1)S(1)}, bf16[64,5376]{1,0:T(8,128)(2,1)S(1)}, u32[]{:S(2)}, u32[]{:S(2)}) collective-permute-start(bf16[64,5376]{1,0:T(8,128)(2,1)S(1)} %get-tuple-element.58), channel_id=1, source_target_pairs={{0,2},{1,3},{2,0},{3,1},{4,6},{5,7},{6,4},{7,5},{8,10},{9,11},{10,... | collective-permute-start | bytes 2064392 | tf_op jit(solution)/shard_map/ppermute | solution.py:53
  199.1 31.8 %collective-permute-start.13 = (bf16[64,5376]{1,0:T(8,128)(2,1)}, bf16[64,5376]{1,0:T(8,128)(2,1)S(1)}, u32[]{:S(2)}, u32[]{:S(2)}) collective-permute-start(bf16[64,5376]{1,0:T(8,128)(2,1)} %get-tuple-element.57), channel_id=1, source_target_pairs={{0,3},{1,0},{2,1},{3,2},{4,7},{5,4},{6,5},{7,6},{8,11},{9,8},{10,9... | collective-permute-start | bytes 2064392 | tf_op jit(solution)/shard_map/ppermute | solution.py:53
  199.1 34.0 %collective-permute-start.14 = (bf16[64,5376]{1,0:T(8,128)(2,1)}, bf16[64,5376]{1,0:T(8,128)(2,1)}, u32[]{:S(2)}, u32[]{:S(2)}) collective-permute-start(bf16[64,5376]{1,0:T(8,128)(2,1)} %get-tuple-element.56), channel_id=1, source_target_pairs={{0,4},{1,5},{2,6},{3,7},{4,0},{5,1},{6,2},{7,3},{8,12},{9,13},{10,... | collective-permute-start | bytes 2064392 | tf_op jit(solution)/shard_map/ppermute | solution.py:53
  199.5 59.6 %collective-permute-start.15 = (bf16[64,5376]{1,0:T(8,128)(2,1)}, bf16[64,5376]{1,0:T(8,128)(2,1)}, u32[]{:S(2)}, u32[]{:S(2)}) collective-permute-start(bf16[64,5376]{1,0:T(8,128)(2,1)} %get-tuple-element.55), channel_id=1, source_target_pairs={{0,5},{1,6},{2,7},{3,4},{4,1},{5,2},{6,3},{7,0},{8,13},{9,14},{10,... | collective-permute-start | bytes 2064392 | tf_op jit(solution)/shard_map/ppermute | solution.py:53
  212.6 76.5 %collective-permute-start.16 = (bf16[64,5376]{1,0:T(8,128)(2,1)}, bf16[64,5376]{1,0:T(8,128)(2,1)}, u32[]{:S(2)}, u32[]{:S(2)}) collective-permute-start(bf16[64,5376]{1,0:T(8,128)(2,1)} %get-tuple-element.54), channel_id=1, source_target_pairs={{0,6},{1,7},{2,4},{3,5},{4,2},{5,3},{6,0},{7,1},{8,14},{9,15},{10,... | collective-permute-start | bytes 2064392 | tf_op jit(solution)/shard_map/ppermute | solution.py:53
  229.1 84.1 %collective-permute-start.17 = (bf16[64,5376]{1,0:T(8,128)(2,1)}, bf16[64,5376]{1,0:T(8,128)(2,1)}, u32[]{:S(2)}, u32[]{:S(2)}) collective-permute-start(bf16[64,5376]{1,0:T(8,128)(2,1)} %get-tuple-element.53), channel_id=1, source_target_pairs={{0,7},{1,4},{2,5},{3,6},{4,3},{5,0},{6,1},{7,2},{8,15},{9,12},{10,... | collective-permute-start | bytes 2064392 | tf_op jit(solution)/shard_map/ppermute | solution.py:53
Sparse Core Ops, SparseCore 0:
  169.3 130.4 reduce-scatter.1

commit v2 on v1

--- a/solution.py
+++ b/solution.py
@@ -52,6 +52,48 @@
         piece = lax.dynamic_index_in_dim(pieces, target, 0, keepdims=False)
         total = total + lax.ppermute(piece, axis, route).astype(jnp.float32)
     return total
+
+
+def ring_scatter_sum(blocks, axis, count, stride, forward):
+    size = lax.axis_size(axis)
+    me = lax.axis_index(axis)
+    digit = (me // stride) % count
+    step = 1 if forward else -1
+    route = [
+        (i, i - ((i // stride) % count) * stride + (((i // stride) % count + step) % count) * stride)
+        for i in range(size)
+    ]
+
+    def chunk(k):
+        return lax.dynamic_index_in_dim(blocks, (digit - step * (k + 1)) % count, 0, keepdims=False)
+
+    running = chunk(0)
+    for k in range(count - 1):
+        running = lax.ppermute(running.astype(jnp.bfloat16), axis, route).astype(jnp.float32) + chunk(k + 1)
+    return running
+
+
+def pair_scatter_sum(blocks, axis, stride):
+    size = lax.axis_size(axis)
+    me = lax.axis_index(axis)
+    digit = (me // stride) % 2
+    route = [(i, i + stride if (i // stride) % 2 == 0 else i - stride) for i in range(size)]
+    own = lax.dynamic_index_in_dim(blocks, digit, 0, keepdims=False)
+    other = lax.dynamic_index_in_dim(blocks, 1 - digit, 0, keepdims=False)
+    return own + lax.ppermute(other.astype(jnp.bfloat16), axis, route).astype(jnp.float32)
+
+
+def ctx_scatter_sum(full, axis, levels):
+    outer, middle, inner = levels
+    width = full.shape[1]
+    grid = full.reshape(outer, middle, inner, -1, width)
+    grid = jnp.moveaxis(grid, 2, 0)
+    grid = pair_scatter_sum(grid, axis, 1)
+    half = width // 2
+    up = ring_scatter_sum(grid[..., :half], axis, outer, middle * inner, True)
+    down = ring_scatter_sum(grid[..., half:], axis, outer, middle * inner, False)
+    grid = jnp.concatenate([up, down], axis=-1)
+    return pair_scatter_sum(grid, axis, inner)
 
 
 def rope_tables(positions, head_size):
@@ -225,20 +267,17 @@
     grad_value = own_pair[1].astype(jnp.bfloat16)
     key_width = key_weight.shape[1]
     query_width = query_weight.shape[1]
-    summed = lax.psum_scatter(
-        (
-            lax.dot_general(
-                gathered,
-                jnp.concatenate([grad_query, grad_key, grad_value], axis=1),
-                contract,
-                preferred_element_type=jnp.float32,
-            )
-            * grad_scale
-        ).astype(jnp.bfloat16),
+    summed = ctx_scatter_sum(
+        lax.dot_general(
+            gathered,
+            jnp.concatenate([grad_query, grad_key, grad_value], axis=1),
+            contract,
+            preferred_element_type=jnp.float32,
+        )
+        * grad_scale,
         "ctx",
-        scatter_dimension=0,
-        tiled=True,
-    ).astype(jnp.float32)
+        (lax.axis_size("ctx") // 4, 2, 2),
+    )
     query_weight_grad = summed[:, :query_width]
     key_weight_grad = summed[:, query_width : query_width + key_width]
     value_weight_grad = summed[:, query_width + key_width :]

time: 331 us -> 325 us (0.982)
  starting transfers between devices: 71 us -> 120 us
  waiting for transfers between devices: 133 us -> 84.6 us
  between operations: 15 us -> 1.68 us
  local copies, waits for them, and re-layouts: 37.5 us -> 44 us
  other arithmetic: 17.7 us -> 23.2 us
  matrix products: 52.6 us -> 47.8 us
    ppermute x7, waiting for transfers between devices: 107 us -> 42.3 us  [scatter_sum_over(): total = total + lax.ppermute(piece, axis, route).astype(jnp.float32)]
    ppermute x0 -> x16, starting transfers between devices: none -> 30 us  [the longest x14 25.7 us: ring_scatter_sum(): lax.ppermute(running.astype(jnp.bfloat16), axis, route).astype(jnp.float32)]
    ppermute x0 -> x16, waiting for transfers between devices: none -> 19.8 us  [the longest x14 19.7 us: ring_scatter_sum(): lax.ppermute(running.astype(jnp.bfloat16), axis, route).astype(jnp.float32)]
    ppermute x4, starting transfers between devices: 10.2 us -> 24.8 us  [passed_along(): return lax.ppermute(block, axis, route)]
    dot_general x1, matrix products: 10.7 us -> 0.58 us  [attend_backward(): jnp.einsum('kgqj,jkd->qkgd', shifts, key_grid, preferred_element_type=jnp...]
    unnamed x63 -> x77, local copies, waits for them, and re-layouts: 15.9 us -> 23.6 us
    add x0 -> x4, other arithmetic: none -> 4.88 us  [the longest x2 2.76 us: pair_scatter_sum(): own + lax.ppermute(other.astype(jnp.bfloat16), axis, route).astype(jnp.fl...]
    ppermute x7, starting transfers between devices: 13.5 us -> 17.9 us  [scatter_sum_over(): total = total + lax.ppermute(piece, axis, route).astype(jnp.float32)]
  transfers between devices with their start and end apart: 19 -> 34, of which waited for: 12 -> 18; matrix products, arithmetic and copies ran while one was open for 16% -> 19% of each run, Pallas kernels for 0% -> 0%
where the time goes in v2:
time: 325 us; the launch traced here: 321 us
  starting transfers between devices  120 us (37%)
  waiting for transfers between devices  84.6 us (26%)
  matrix products  47.8 us (15%)
  local copies, waits for them, and re-layouts  44 us (14%)
  other arithmetic  23.2 us (7%)
    ppermute x7, starting transfers between devices, gather_over(): lax.ppermute(block, axis, route)  47.2 us
    ppermute x7, waiting for transfers between devices, scatter_sum_over(): total = total + lax.ppermute(piece, axis, route).astype(jnp.float32)  42.3 us
    ppermute x14, starting transfers between devices, ring_scatter_sum(): lax.ppermute(running.astype(jnp.bfloat16), axis, route).astype(jnp.float32)  25.7 us
    ppermute x4, starting transfers between devices, passed_along(): return lax.ppermute(block, axis, route)  24.8 us
    unnamed x77, local copies, waits for them, and re-layouts  23.6 us
    ppermute x14, waiting for transfers between devices, ring_scatter_sum(): lax.ppermute(running.astype(jnp.bfloat16), axis, route).astype(jnp.float32)  19.7 us
    ppermute x7, starting transfers between devices, scatter_sum_over(): total = total + lax.ppermute(piece, axis, route).astype(jnp.float32)  17.9 us
    ppermute x4, waiting for transfers between devices, passed_along(): return lax.ppermute(block, axis, route)  14.1 us
  transfers between devices with their start and end apart: 34, of which 18 were waited for; matrix products, arithmetic and copies ran while one was open for 19% of the time, Pallas kernels for 0%

profile of v2, /device:TPU:96, one launch (start us, length us, event | category | flops | bytes accessed | tf_op | source)
XLA Modules:
  0.0 321.1 jit_solution(2229688004234722770)
XLA Ops:
  0.7 1.7 collective-permute-start
  2.3 2.9 collective-permute-start.1
  5.2 1.3 collective-permute-start.2
  6.6 3.0 collective-permute-start.3
  10.2 2.1 bitcast_dynamic-update-slice_fusion.7
  14.5 4.5 %copy.41 = bf16[256,5376]{1,0:T(8,128)(2,1)} copy(bf16[256,5376]{0,1:T(8,128)(2,1)} %bitcast.271) | data formatting | bytes 5505024 | tf_op jit(solution)/shard_map/dot_general | solution.py:203
  21.2 1.9 fusion.7
  23.1 37.6 %collective-permute-start.5 = (bf16[64,5376]{1,0:T(8,128)(2,1)S(1)}, bf16[64,5376]{1,0:T(8,128)(2,1)S(1)}, u32[]{:S(2)}, u32[]{:S(2)}) collective-permute-start(bf16[64,5376]{1,0:T(8,128)(2,1)S(1)} %copy-done.17), channel_id=1, source_target_pairs={{0,6},{1,7},{2,4},{3,5},{4,2},{5,3},{6,0},{7,1},{8,14},{9,15},{10,... | collective-permute-start | bytes 2064392 | tf_op jit(solution)/shard_map/ppermute | solution.py:42
  60.8 2.0 bitcast_dynamic-update-slice_fusion.6
  62.8 2.0 bitcast_dynamic-update-slice_fusion.5
  64.8 2.0 bitcast_dynamic-update-slice_fusion.4
  66.8 2.0 bitcast_dynamic-update-slice_fusion.3
  69.7 5.6 %collective-permute-done.5 = bf16[64,5376]{1,0:T(8,128)(2,1)S(1)} collective-permute-done((bf16[64,5376]{1,0:T(8,128)(2,1)S(1)}, bf16[64,5376]{1,0:T(8,128)(2,1)S(1)}, u32[]{:S(2)}, u32[]{:S(2)}) %collective-permute-start.5) | collective-permute-done | bytes 688160 | tf_op jit(solution)/shard_map/ppermute | solution.py:42
  76.2 2.9 collective-permute-done.6
  80.0 5.9 %gather_fusion = bf16[8,64,5376]{2,1,0:T(8,128)(2,1)} fusion(bf16[8,64,5376]{2,1,0:T(8,128)(2,1)} %bitcast_dynamic-update-slice_fusion, s32[1024]{0:T(1024)} %pad_clamp_fusion), kind=kCustom, calls=%fused_computation | custom fusion | bytes 11010080 | tf_op jit(solution)/shard_map/jit(_take)/gather | solution.py:44
  85.9 3.1 bitcast_select_fusion.1
  89.1 2.0 multiply_reduce_fusion.3
  91.8 1.9 fusion.17
  93.8 3.7 %collective-permute-start.7 = (bf16[2,512,128]{1,2,0:T(8,128)(2,1)S(1)}, bf16[2,512,128]{1,2,0:T(8,128)(2,1)S(1)}, u32[]{:S(2)}, u32[]{:S(2)}) collective-permute-start(bf16[2,512,128]{1,2,0:T(8,128)(2,1)S(1)} %pad_maximum_fusion.1), channel_id=1, source_target_pairs={{0,16},{8,24},{16,32},{24,40},{32,48},{40,56},{48,64},{56,72},{64,... | collective-permute-start | bytes 786440 | tf_op jit(solution)/shard_map/ppermute | solution.py:18
  97.5 14.3 %collective-permute-start.8 = (bf16[2,512,128]{1,2,0:T(8,128)(2,1)S(1)}, bf16[2,512,128]{1,2,0:T(8,128)(2,1)S(1)}, u32[]{:S(2)}, u32[]{:S(2)}) collective-permute-start(bf16[2,512,128]{1,2,0:T(8,128)(2,1)S(1)} %pad_maximum_fusion.1), channel_id=1, source_target_pairs={{0,8},{8,16},{16,24},{24,32},{32,40},{40,48},{48,56},{56,64},{64,7... | collective-permute-start | bytes 786440 | tf_op jit(solution)/shard_map/ppermute | solution.py:18
  112.5 1.6 multiply_reduce_fusion.2
  117.1 2.9 bitcast_convert_fusion.1
  119.9 3.0 convolution_bitcast_fusion
  123.0 2.0 copy.35
  125.0 2.4 multiply_reduce_fusion
  128.5 5.3 %fusion.4 = bf16[2,512,1536]{1,2,0:T(8,128)(2,1)S(1)} fusion(bf16[512,2,128]{0,2,1:T(8,128)(2,1)} %copy.22, f32[1536,512,2]{1,0,2:T(8,128)} %copy-done.3, f32[2,512]{1,0:T(2,128)S(1)} %copy.36, f32[2,512]{1,0:T(2,128)S(1)} %log_add_fusion, pred[512,1536]{0,1:T(8,128)(4,1)S(1)} %fusion.7, bf16[2,1536,128]{1,2,0:T(8,128)(2,1)} %copy-done.8), kind=kOutput, calls=%fused_computation.17 | convolution fusion | flops 412090368 | bytes 10887168 | tf_op jit(solution)/shard_map/while/body/eval_jaxpr/qkgd,jkd->kgqj/dot_general | solution.py:175
  135.7 3.5 %collective-permute-start.10 = (f32[2,512,128]{1,2,0:T(8,128)S(1)}, f32[2,512,128]{1,2,0:T(8,128)S(1)}, u32[]{:S(2)}, u32[]{:S(2)}) collective-permute-start(f32[2,512,128]{1,2,0:T(8,128)S(1)} %get-tuple-element.73), channel_id=1, source_target_pairs={{16,0},{24,8},{32,16},{40,24},{48,32},{56,40},{64,48},{72,56},{80,... | collective-permute-start | bytes 1572872 | tf_op jit(solution)/shard_map/ppermute | solution.py:18
  139.2 3.4 %collective-permute-start.9 = (f32[2,512,128]{1,2,0:T(8,128)S(1)}, f32[2,512,128]{1,2,0:T(8,128)S(1)}, u32[]{:S(2)}, u32[]{:S(2)}) collective-permute-start(f32[2,512,128]{1,2,0:T(8,128)S(1)} %get-tuple-element.72), channel_id=1, source_target_pairs={{8,0},{16,8},{24,16},{32,24},{40,32},{48,40},{56,48},{64,56},{72,6... | collective-permute-start | bytes 1572872 | tf_op jit(solution)/shard_map/ppermute | solution.py:18
  143.0 9.5 %collective-permute-done.10 = f32[2,512,128]{1,2,0:T(8,128)S(1)} collective-permute-done((f32[2,512,128]{1,2,0:T(8,128)S(1)}, f32[2,512,128]{1,2,0:T(8,128)S(1)}, u32[]{:S(2)}, u32[]{:S(2)}) %collective-permute-start.10) | collective-permute-done | bytes 524320 | tf_op jit(solution)/shard_map/ppermute | solution.py:18
  152.5 4.6 %collective-permute-done.9 = f32[2,512,128]{1,2,0:T(8,128)S(1)} collective-permute-done((f32[2,512,128]{1,2,0:T(8,128)S(1)}, f32[2,512,128]{1,2,0:T(8,128)S(1)}, u32[]{:S(2)}, u32[]{:S(2)}) %collective-permute-start.9) | collective-permute-done | bytes 524320 | tf_op jit(solution)/shard_map/ppermute | solution.py:18
  158.1 3.1 convolution_multiply_fusion
  161.3 4.1 %copy-done.2 = f32[5376,512]{1,0:T(8,128)} copy-done((f32[5376,512]{1,0:T(8,128)}, f32[5376,512]{1,0:T(8,128)S(1)}, u32[]{:S(2)}) %copy-start.2) | copy-done | bytes 11010072
  165.4 2.0 fusion.8
  167.4 2.3 collective-permute-start.18
  169.7 7.5 %fusion.84 = f32[512,5376]{1,0:T(8,128)} fusion(bf16[512,256]{0,1:T(8,128)(2,1)S(1)} %bitcast.275, bf16[5376,256]{1,0:T(8,128)(2,1)} %param.8), kind=kOutput, calls=%fused_computation.179 | convolution fusion | flops 1409286144 | bytes 14024704 | tf_op jit(solution)/shard_map/dot_general | solution.py:285
  177.2 5.6 %fusion.85 = f32[512,5376]{1,0:T(8,128)} fusion(bf16[512,128]{0,1:T(8,128)(2,1)S(1)} %fusion.67, bf16[5376,128]{1,0:T(8,128)(2,1)S(1)} %copy-done), kind=kOutput, calls=%fused_computation.180 | convolution fusion | flops 704643072 | bytes 12517376 | tf_op jit(solution)/shard_map/dot_general | solution.py:288
  182.8 11.8 %add_convert_fusion = bf16[512,5376]{1,0:T(8,128)(2,1)} fusion(f32[512,5376]{1,0:T(8,128)} %fusion.84, f32[512,5376]{1,0:T(8,128)} %fusion.85, bf16[5376,128]{1,0:T(8,128)(2,1)} %param.10, f32[2,512,128]{1,2,0:T(8,128)S(1)} %fusion.22), kind=kOutput, calls=%fused_computation.1 | convolution fusion | flops 712900608 | bytes 29032448 | tf_op jit(solution)/shard_map/dot_general | solution.py:294
  194.7 2.7 bitcast_add_fusion
  198.3 3.6 %copy-done.4 = bf16[512,5376]{1,0:T(8,128)(2,1)S(1)} copy-done((bf16[512,5376]{1,0:T(8,128)(2,1)S(1)}, bf16[512,5376]{1,0:T(8,128)(2,1)}, u32[]{:S(2)}) %copy-start.4) | copy-done | bytes 5505048
  201.9 1.9 dynamic-slice_bitcast_fusion.6
  203.8 3.6 %collective-permute-start.11 = (bf16[64,5376]{1,0:T(8,128)(2,1)S(1)}, bf16[64,5376]{1,0:T(8,128)(2,1)S(1)}, u32[]{:S(2)}, u32[]{:S(2)}) collective-permute-start(bf16[64,5376]{1,0:T(8,128)(2,1)S(1)} %get-tuple-element.54), channel_id=1, source_target_pairs={{0,1},{1,2},{2,3},{3,0},{4,5},{5,6},{6,7},{7,4},{8,9},{9,10},{10,1... | collective-permute-start | bytes 2064392 | tf_op jit(solution)/shard_map/ppermute | solution.py:53
  207.4 4.1 %collective-permute-start.12 = (bf16[64,5376]{1,0:T(8,128)(2,1)S(1)}, bf16[64,5376]{1,0:T(8,128)(2,1)S(1)}, u32[]{:S(2)}, u32[]{:S(2)}) collective-permute-start(bf16[64,5376]{1,0:T(8,128)(2,1)S(1)} %get-tuple-element.60), channel_id=1, source_target_pairs={{0,2},{1,3},{2,0},{3,1},{4,6},{5,7},{6,4},{7,5},{8,10},{9,11},{10,... | collective-permute-start | bytes 2064392 | tf_op jit(solution)/shard_map/ppermute | solution.py:53
  211.5 2.6 collective-permute-start.19
  214.3 3.5 %collective-permute-done.19 = bf16[2,168,256]{2,1,0:T(8,128)(2,1)S(1)} collective-permute-done((bf16[2,168,256]{2,1,0:T(8,128)(2,1)S(1)}, bf16[2,168,256]{2,1,0:T(8,128)(2,1)S(1)}, u32[]{:S(2)}, u32[]{:S(2)}) %collective-permute-start.19) | collective-permute-done | bytes 172064 | tf_op jit(solution)/shard_map/ppermute | solution.py:72
  217.8 3.4 %collective-permute-start.20 = (bf16[2,168,256]{2,1,0:T(8,128)(2,1)S(1)}, bf16[2,168,256]{2,1,0:T(8,128)(2,1)S(1)}, u32[]{:S(2)}, u32[]{:S(2)}) collective-permute-start(bf16[2,168,256]{2,1,0:T(8,128)(2,1)S(1)} %fusion.46), channel_id=1, source_target_pairs={{0,32},{8,40},{16,48},{24,56},{32,64},{40,72},{48,80},{56,88},{64,... | collective-permute-start | bytes 516104 | tf_op jit(solution)/shard_map/ppermute | solution.py:72
  221.5 2.6 collective-permute-done.20
  224.2 3.8 %collective-permute-start.21 = (bf16[2,168,256]{2,1,0:T(8,128)(2,1)S(1)}, bf16[2,168,256]{2,1,0:T(8,128)(2,1)S(1)}, u32[]{:S(2)}, u32[]{:S(2)}) collective-permute-start(bf16[2,168,256]{2,1,0:T(8,128)(2,1)S(1)} %fusion.45), channel_id=1, source_target_pairs={{0,32},{8,40},{16,48},{24,56},{32,64},{40,72},{48,80},{56,88},{64,... | collective-permute-start | bytes 516104 | tf_op jit(solution)/shard_map/ppermute | solution.py:72
  228.3 2.6 collective-permute-done.21
  230.9 3.8 %collective-permute-start.22 = (bf16[2,168,256]{2,1,0:T(8,128)(2,1)S(1)}, bf16[2,168,256]{2,1,0:T(8,128)(2,1)S(1)}, u32[]{:S(2)}, u32[]{:S(2)}) collective-permute-start(bf16[2,168,256]{2,1,0:T(8,128)(2,1)S(1)} %fusion.44), channel_id=1, source_target_pairs={{0,32},{8,40},{16,48},{24,56},{32,64},{40,72},{48,80},{56,88},{64,... | collective-permute-start | bytes 516104 | tf_op jit(solution)/shard_map/ppermute | solution.py:72
  235.0 2.6 collective-permute-done.22
  237.7 3.8 %collective-permute-start.23 = (bf16[2,168,256]{2,1,0:T(8,128)(2,1)S(1)}, bf16[2,168,256]{2,1,0:T(8,128)(2,1)S(1)}, u32[]{:S(2)}, u32[]{:S(2)}) collective-permute-start(bf16[2,168,256]{2,1,0:T(8,128)(2,1)S(1)} %fusion.43), channel_id=1, source_target_pairs={{0,32},{8,40},{16,48},{24,56},{32,64},{40,72},{48,80},{56,88},{64,... | collective-permute-start | bytes 516104 | tf_op jit(solution)/shard_map/ppermute | solution.py:72
  242.1 3.2 collective-permute-done.23
  245.3 3.8 %collective-permute-start.24 = (bf16[2,168,256]{2,1,0:T(8,128)(2,1)S(1)}, bf16[2,168,256]{2,1,0:T(8,128)(2,1)S(1)}, u32[]{:S(2)}, u32[]{:S(2)}) collective-permute-start(bf16[2,168,256]{2,1,0:T(8,128)(2,1)S(1)} %fusion.42), channel_id=1, source_target_pairs={{0,32},{8,40},{16,48},{24,56},{32,64},{40,72},{48,80},{56,88},{64,... | collective-permute-start | bytes 516104 | tf_op jit(solution)/shard_map/ppermute | solution.py:72
  250.2 3.4 %collective-permute-done.24 = bf16[2,168,256]{2,1,0:T(8,128)(2,1)S(1)} collective-permute-done((bf16[2,168,256]{2,1,0:T(8,128)(2,1)S(1)}, bf16[2,168,256]{2,1,0:T(8,128)(2,1)S(1)}, u32[]{:S(2)}, u32[]{:S(2)}) %collective-permute-start.24) | collective-permute-done | bytes 172064 | tf_op jit(solution)/shard_map/ppermute | solution.py:72
  253.7 3.8 %collective-permute-start.25 = (bf16[2,168,256]{2,1,0:T(8,128)(2,1)S(1)}, bf16[2,168,256]{2,1,0:T(8,128)(2,1)}, u32[]{:S(2)}, u32[]{:S(2)}) collective-permute-start(bf16[2,168,256]{2,1,0:T(8,128)(2,1)S(1)} %fusion.41), channel_id=1, source_target_pairs={{0,32},{8,40},{16,48},{24,56},{32,64},{40,72},{48,80},{56,88},{64,... | collective-permute-start | bytes 516104 | tf_op jit(solution)/shard_map/ppermute | solution.py:72
  258.4 4.1 %collective-permute-start.15 = (bf16[64,5376]{1,0:T(8,128)(2,1)}, bf16[64,5376]{1,0:T(8,128)(2,1)}, u32[]{:S(2)}, u32[]{:S(2)}) collective-permute-start(bf16[64,5376]{1,0:T(8,128)(2,1)} %get-tuple-element.57), channel_id=1, source_target_pairs={{0,5},{1,6},{2,7},{3,4},{4,1},{5,2},{6,3},{7,0},{8,13},{9,14},{10,... | collective-permute-start | bytes 2064392 | tf_op jit(solution)/shard_map/ppermute | solution.py:53
  263.3 4.5 %collective-permute-start.17 = (bf16[64,5376]{1,0:T(8,128)(2,1)}, bf16[64,5376]{1,0:T(8,128)(2,1)}, u32[]{:S(2)}, u32[]{:S(2)}) collective-permute-start(bf16[64,5376]{1,0:T(8,128)(2,1)} %get-tuple-element.55), channel_id=1, source_target_pairs={{0,7},{1,4},{2,5},{3,6},{4,3},{5,0},{6,1},{7,2},{8,15},{9,12},{10,... | collective-permute-start | bytes 2064392 | tf_op jit(solution)/shard_map/ppermute | solution.py:53
  267.8 1.8 copy.24
  271.7 2.0 collective-permute-start.33
  273.7 3.9 %collective-permute-done.14 = bf16[64,5376]{1,0:T(8,128)(2,1)} collective-permute-done((bf16[64,5376]{1,0:T(8,128)(2,1)}, bf16[64,5376]{1,0:T(8,128)(2,1)}, u32[]{:S(2)}, u32[]{:S(2)}) %collective-permute-start.14) | collective-permute-done | bytes 688160 | tf_op jit(solution)/shard_map/ppermute | solution.py:53
  277.6 15.3 %collective-permute-done.15 = bf16[64,5376]{1,0:T(8,128)(2,1)} collective-permute-done((bf16[64,5376]{1,0:T(8,128)(2,1)}, bf16[64,5376]{1,0:T(8,128)(2,1)}, u32[]{:S(2)}, u32[]{:S(2)}) %collective-permute-start.15) | collective-permute-done | bytes 688160 | tf_op jit(solution)/shard_map/ppermute | solution.py:53
  293.0 15.9 %collective-permute-done.16 = bf16[64,5376]{1,0:T(8,128)(2,1)} collective-permute-done((bf16[64,5376]{1,0:T(8,128)(2,1)}, bf16[64,5376]{1,0:T(8,128)(2,1)}, u32[]{:S(2)}, u32[]{:S(2)}) %collective-permute-start.16) | collective-permute-done | bytes 688160 | tf_op jit(solution)/shard_map/ppermute | solution.py:53
  308.8 7.2 %collective-permute-done.17 = bf16[64,5376]{1,0:T(8,128)(2,1)} collective-permute-done((bf16[64,5376]{1,0:T(8,128)(2,1)}, bf16[64,5376]{1,0:T(8,128)(2,1)}, u32[]{:S(2)}, u32[]{:S(2)}) %collective-permute-start.17) | collective-permute-done | bytes 688160 | tf_op jit(solution)/shard_map/ppermute | solution.py:53
  316.0 3.5 %fusion.15 = bf16[64,5376]{1,0:T(8,128)(2,1)} fusion(bf16[64,5376]{1,0:T(8,128)(2,1)} %collective-permute-done.17, bf16[64,5376]{1,0:T(8,128)(2,1)} %collective-permute-done.16, bf16[64,5376]{1,0:T(8,128)(2,1)} %collective-permute-done.15, bf16[64,5376]{1,0:T(8,128)(2,1)} %collective-permute-done.14, bf16[64,5376]{1,0:T(8,128)(2,1)S(1)} %collective-permute-done.13, ...), kind=kLoop, calls=%fused_computation.35 | loop fusion | flops 5505024 | bytes 6193156 | tf_op jit(solution)/shard_map/convert_element_type | solution.py:299
  (168 shorter events, 25.5 us)
Async XLA Ops:
  0.6 88.4 %copy-start = (bf16[5376,128]{1,0:T(8,128)(2,1)S(1)}, bf16[5376,128]{1,0:T(8,128)(2,1)}, u32[]{:S(2)}) copy-start(bf16[5376,128]{1,0:T(8,128)(2,1)} %param.9) | copy-start | bytes 4128772
  0.6 22.5 %copy-start.17 = (bf16[64,5376]{1,0:T(8,128)(2,1)S(1)}, bf16[64,5376]{1,0:T(8,128)(2,1)}, u32[]{:S(2)}) copy-start(bf16[64,5376]{1,0:T(8,128)(2,1)} %param.7) | copy-start | bytes 2064388
  0.7 18.3 %copy-start.18 = (bf16[512,256]{1,0:T(8,128)(2,1)S(1)}, bf16[512,256]{1,0:T(8,128)(2,1)}, u32[]{:S(2)}) copy-start(bf16[512,256]{1,0:T(8,128)(2,1)} %param.13) | copy-start | bytes 786436
  0.7 22.4 %collective-permute-start = (bf16[64,5376]{1,0:T(8,128)(2,1)}, bf16[64,5376]{1,0:T(8,128)(2,1)}, u32[]{:S(2)}, u32[]{:S(2)}) collective-permute-start(bf16[64,5376]{1,0:T(8,128)(2,1)} %param.7), channel_id=1, source_target_pairs={{0,1},{1,2},{2,3},{3,0},{4,5},{5,6},{6,7},{7,4},{8,9},{9,10},{10,1... | collective-permute-start | bytes 2064392 | tf_op jit(solution)/shard_map/ppermute | solution.py:42
  2.3 60.4 %collective-permute-start.1 = (bf16[64,5376]{1,0:T(8,128)(2,1)}, bf16[64,5376]{1,0:T(8,128)(2,1)}, u32[]{:S(2)}, u32[]{:S(2)}) collective-permute-start(bf16[64,5376]{1,0:T(8,128)(2,1)} %param.7), channel_id=1, source_target_pairs={{0,2},{1,3},{2,0},{3,1},{4,6},{5,7},{6,4},{7,5},{8,10},{9,11},{10,... | collective-permute-start | bytes 2064392 | tf_op jit(solution)/shard_map/ppermute | solution.py:42
  5.2 59.5 %collective-permute-start.2 = (bf16[64,5376]{1,0:T(8,128)(2,1)}, bf16[64,5376]{1,0:T(8,128)(2,1)}, u32[]{:S(2)}, u32[]{:S(2)}) collective-permute-start(bf16[64,5376]{1,0:T(8,128)(2,1)} %param.7), channel_id=1, source_target_pairs={{0,3},{1,0},{2,1},{3,2},{4,7},{5,4},{6,5},{7,6},{8,11},{9,8},{10,9... | collective-permute-start | bytes 2064392 | tf_op jit(solution)/shard_map/ppermute | solution.py:42
  6.6 60.2 %collective-permute-start.3 = (bf16[64,5376]{1,0:T(8,128)(2,1)}, bf16[64,5376]{1,0:T(8,128)(2,1)}, u32[]{:S(2)}, u32[]{:S(2)}) collective-permute-start(bf16[64,5376]{1,0:T(8,128)(2,1)} %param.7), channel_id=1, source_target_pairs={{0,4},{1,5},{2,6},{3,7},{4,0},{5,1},{6,2},{7,3},{8,12},{9,13},{10,... | collective-permute-start | bytes 2064392 | tf_op jit(solution)/shard_map/ppermute | solution.py:42
  9.6 59.2 %collective-permute-start.4 = (bf16[64,5376]{1,0:T(8,128)(2,1)}, bf16[64,5376]{1,0:T(8,128)(2,1)S(1)}, u32[]{:S(2)}, u32[]{:S(2)}) collective-permute-start(bf16[64,5376]{1,0:T(8,128)(2,1)} %param.7), channel_id=1, source_target_pairs={{0,5},{1,6},{2,7},{3,4},{4,1},{5,2},{6,3},{7,0},{8,13},{9,14},{10,... | collective-permute-start | bytes 2064392 | tf_op jit(solution)/shard_map/ppermute | solution.py:42
  12.3 7.7 %copy-start.21 = (f32[64]{0:T(128)}, f32[64]{0:T(128)S(1)}, u32[]{:S(2)}) copy-start(f32[64]{0:T(128)S(1)} %multiply_exponential_fusion) | copy-start | bytes 772
  13.7 6.2 %copy-start.24 = (pred[8]{0:T(512)(128)(4,1)}, pred[8]{0:T(512)(128)(4,1)S(1)}, u32[]{:S(2)}) copy-start(pred[8]{0:T(512)(128)(4,1)S(1)} %compare_and_fusion) | copy-start | bytes 28
  23.1 52.2 %collective-permute-start.5 = (bf16[64,5376]{1,0:T(8,128)(2,1)S(1)}, bf16[64,5376]{1,0:T(8,128)(2,1)S(1)}, u32[]{:S(2)}, u32[]{:S(2)}) collective-permute-start(bf16[64,5376]{1,0:T(8,128)(2,1)S(1)} %copy-done.17), channel_id=1, source_target_pairs={{0,6},{1,7},{2,4},{3,5},{4,2},{5,3},{6,0},{7,1},{8,14},{9,15},{10,... | collective-permute-start | bytes 2064392 | tf_op jit(solution)/shard_map/ppermute | solution.py:42
  62.8 16.3 %collective-permute-start.6 = (bf16[64,5376]{1,0:T(8,128)(2,1)S(1)}, bf16[64,5376]{1,0:T(8,128)(2,1)S(1)}, u32[]{:S(2)}, u32[]{:S(2)}) collective-permute-start(bf16[64,5376]{1,0:T(8,128)(2,1)S(1)} %copy-done.17), channel_id=1, source_target_pairs={{0,7},{1,4},{2,5},{3,6},{4,3},{5,0},{6,1},{7,2},{8,15},{9,12},{10,... | collective-permute-start | bytes 2064392 | tf_op jit(solution)/shard_map/ppermute | solution.py:42
  80.0 5.9 %copy-start.26 = (pred[512]{0:T(512)(128)(4,1)S(1)}, pred[512]{0:T(512)(128)(4,1)}, u32[]{:S(2)}) copy-start(pred[512]{0:T(512)(128)(4,1)} %broadcast_in_dim.84) | copy-start | bytes 1540
  89.0 4.7 %copy-start.1 = (bf16[512,5376]{1,0:T(8,128)(2,1)}, bf16[512,5376]{1,0:T(8,128)(2,1)S(1)}, u32[]{:S(2)}) copy-start(bf16[512,5376]{1,0:T(8,128)(2,1)S(1)} %bitcast_select_fusion.1) | copy-start | bytes 16515076
  89.0 2.0 copy-start.23
  89.0 2.1 copy-start.22
  89.1 2.7 copy-start.7
  91.2 20.6 %slice-start.2 = ((s8[5505024]{0:T(1024)(128)(4,1)}), s8[4194304]{0:T(1024)(128)(4,1)S(1)}, s32[]{:S(2)}) async-start(s8[5505024]{0:T(1024)(128)(4,1)} %bitcast.263), calls=%async_computation.2 | async-start | bytes 8388608
  91.2 20.6 %copy-start.25 = (pred[8]{0:T(512)(128)(4,1)S(1)}, pred[8]{0:T(512)(128)(4,1)}, u32[]{:S(2)}) copy-start(pred[8]{0:T(512)(128)(4,1)} %copy-done.24) | copy-start | bytes 28
  91.8 20.0 %slice-start.3 = ((s8[5505024]{0:T(1024)(128)(4,1)}), s8[1310720]{0:T(1024)(128)(4,1)S(1)}, s32[]{:S(2)}) async-start(s8[5505024]{0:T(1024)(128)(4,1)} %bitcast.263), calls=%async_computation.3 | async-start | bytes 2621440
  93.8 18.6 %copy-start.11 = (bf16[256,5376]{1,0:T(8,128)(2,1)S(1)}, bf16[256,5376]{1,0:T(8,128)(2,1)}, u32[]{:S(2)}) copy-start(bf16[256,5376]{1,0:T(8,128)(2,1)} %copy.41) | copy-start | bytes 8257540
  93.8 20.5 %collective-permute-start.7 = (bf16[2,512,128]{1,2,0:T(8,128)(2,1)S(1)}, bf16[2,512,128]{1,2,0:T(8,128)(2,1)S(1)}, u32[]{:S(2)}, u32[]{:S(2)}) collective-permute-start(bf16[2,512,128]{1,2,0:T(8,128)(2,1)S(1)} %pad_maximum_fusion.1), channel_id=1, source_target_pairs={{0,16},{8,24},{16,32},{24,40},{32,48},{40,56},{48,64},{56,72},{64,... | collective-permute-start | bytes 786440 | tf_op jit(solution)/shard_map/ppermute | solution.py:18
  97.5 16.9 %collective-permute-start.8 = (bf16[2,512,128]{1,2,0:T(8,128)(2,1)S(1)}, bf16[2,512,128]{1,2,0:T(8,128)(2,1)S(1)}, u32[]{:S(2)}, u32[]{:S(2)}) collective-permute-start(bf16[2,512,128]{1,2,0:T(8,128)(2,1)S(1)} %pad_maximum_fusion.1), channel_id=1, source_target_pairs={{0,8},{8,16},{16,24},{24,32},{32,40},{40,48},{48,56},{56,64},{64,7... | collective-permute-start | bytes 786440 | tf_op jit(solution)/shard_map/ppermute | solution.py:18
  114.4 2.6 copy-start.8
  115.7 4.2 %copy-start.3 = (f32[1536,512,2]{1,0,2:T(8,128)}, f32[1536,512,2]{1,0,2:T(8,128)S(1)}, u32[]{:S(2)}) copy-start(f32[1536,512,2]{1,0,2:T(8,128)S(1)} %get-tuple-element.91) | copy-start | bytes 18874372
  117.1 2.9 copy-start.19
  128.5 6.5 %copy-start.9 = (bf16[2,1536,128]{1,2,0:T(8,128)(2,1)S(1)}, bf16[2,1536,128]{1,2,0:T(8,128)(2,1)}, u32[]{:S(2)}) copy-start(bf16[2,1536,128]{1,2,0:T(8,128)(2,1)} %copy-done.8) | copy-start | bytes 2359300
  133.8 1.8 copy-start.10
  133.8 8.7 %copy-start.14 = (f32[512,64]{0,1:T(8,128)S(1)}, f32[512,64]{0,1:T(8,128)}, u32[]{:S(2)}) copy-start(f32[512,64]{0,1:T(8,128)} %get-tuple-element.84) | copy-start | bytes 393220
  133.8 8.7 %copy-start.16 = (f32[512,64]{0,1:T(8,128)S(1)}, f32[512,64]{0,1:T(8,128)}, u32[]{:S(2)}) copy-start(f32[512,64]{0,1:T(8,128)} %get-tuple-element.85) | copy-start | bytes 393220
  135.0 23.1 %slice-start = ((s8[5505024]{0:T(1024)(128)(4,1)}), s8[4194304]{0:T(1024)(128)(4,1)S(1)}, s32[]{:S(2)}) async-start(s8[5505024]{0:T(1024)(128)(4,1)} %bitcast.261), calls=%async_computation | async-start | bytes 8388608
  135.7 16.7 %collective-permute-start.10 = (f32[2,512,128]{1,2,0:T(8,128)S(1)}, f32[2,512,128]{1,2,0:T(8,128)S(1)}, u32[]{:S(2)}, u32[]{:S(2)}) collective-permute-start(f32[2,512,128]{1,2,0:T(8,128)S(1)} %get-tuple-element.73), channel_id=1, source_target_pairs={{16,0},{24,8},{32,16},{40,24},{48,32},{56,40},{64,48},{72,56},{80,... | collective-permute-start | bytes 1572872 | tf_op jit(solution)/shard_map/ppermute | solution.py:18
  139.2 17.9 %collective-permute-start.9 = (f32[2,512,128]{1,2,0:T(8,128)S(1)}, f32[2,512,128]{1,2,0:T(8,128)S(1)}, u32[]{:S(2)}, u32[]{:S(2)}) collective-permute-start(f32[2,512,128]{1,2,0:T(8,128)S(1)} %get-tuple-element.72), channel_id=1, source_target_pairs={{8,0},{16,8},{24,16},{32,24},{40,32},{48,40},{56,48},{64,56},{72,6... | collective-permute-start | bytes 1572872 | tf_op jit(solution)/shard_map/ppermute | solution.py:18
  142.7 15.5 %slice-start.1 = ((s8[5505024]{0:T(1024)(128)(4,1)}), s8[1310720]{0:T(1024)(128)(4,1)S(1)}, s32[]{:S(2)}) async-start(s8[5505024]{0:T(1024)(128)(4,1)} %bitcast.261), calls=%async_computation.1 | async-start | bytes 2621440
  161.2 4.1 %copy-start.2 = (f32[5376,512]{1,0:T(8,128)}, f32[5376,512]{1,0:T(8,128)S(1)}, u32[]{:S(2)}) copy-start(f32[5376,512]{1,0:T(8,128)S(1)} %convolution_multiply_fusion) | copy-start | bytes 33030148
  167.4 27.3 %collective-permute-start.18 = (bf16[8,2,168,512]{3,2,1,0:T(8,128)(2,1)}, bf16[8,2,168,512]{3,2,1,0:T(8,128)(2,1)}, u32[]{:S(2)}, u32[]{:S(2)}) collective-permute-start(bf16[8,2,168,512]{3,2,1,0:T(8,128)(2,1)} %fusion.8), channel_id=1, source_target_pairs={{0,8},{8,0},{16,24},{24,16},{32,40},{40,32},{48,56},{56,48},{64,72... | collective-permute-start | bytes 8257544 | tf_op jit(solution)/shard_map/ppermute | solution.py:83
  177.2 17.5 %slice-start.4 = ((s8[11010048]{0:T(1024)(128)(4,1)}), s8[4194304]{0:T(1024)(128)(4,1)S(1)}, s32[]{:S(2)}) async-start(s8[11010048]{0:T(1024)(128)(4,1)} %bitcast.266), calls=%async_computation.4 | async-start | bytes 8388608
  182.8 11.8 %slice-start.5 = ((s8[11010048]{0:T(1024)(128)(4,1)}), s8[4194304]{0:T(1024)(128)(4,1)S(1)}, s32[]{:S(2)}) async-start(s8[11010048]{0:T(1024)(128)(4,1)} %bitcast.266), calls=%async_computation.5 | async-start | bytes 8388608
  182.8 11.8 %slice-start.6 = ((s8[11010048]{0:T(1024)(128)(4,1)}), s8[2621440]{0:T(1024)(128)(4,1)S(1)}, s32[]{:S(2)}) async-start(s8[11010048]{0:T(1024)(128)(4,1)} %bitcast.266), calls=%async_computation.6 | async-start | bytes 5242880
  197.4 4.5 %copy-start.4 = (bf16[512,5376]{1,0:T(8,128)(2,1)S(1)}, bf16[512,5376]{1,0:T(8,128)(2,1)}, u32[]{:S(2)}) copy-start(bf16[512,5376]{1,0:T(8,128)(2,1)} %add_convert_fusion) | copy-start | bytes 16515076
  198.2 51.9 %copy-start.6 = (f32[8,2,168,256]{3,2,1,0:T(8,128)}, f32[8,2,168,256]{3,2,1,0:T(8,128)S(1)}, u32[]{:S(2)}) copy-start(f32[8,2,168,256]{3,2,1,0:T(8,128)S(1)} %get-tuple-element.52) | copy-start | bytes 8257540
  198.2 55.5 %copy-start.5 = (f32[8,2,168,256]{3,2,1,0:T(8,128)}, f32[8,2,168,256]{3,2,1,0:T(8,128)S(1)}, u32[]{:S(2)}) copy-start(f32[8,2,168,256]{3,2,1,0:T(8,128)S(1)} %get-tuple-element.53) | copy-start | bytes 8257540
  198.2 15.9 %collective-permute-start.26 = (bf16[2,168,256]{2,1,0:T(8,128)(2,1)S(1)}, bf16[2,168,256]{2,1,0:T(8,128)(2,1)S(1)}, u32[]{:S(2)}, u32[]{:S(2)}) collective-permute-start(bf16[2,168,256]{2,1,0:T(8,128)(2,1)S(1)} %fusion.58), channel_id=1, source_target_pairs={{0,224},{8,232},{16,240},{24,248},{32,0},{40,8},{48,16},{56,24},{6... | collective-permute-start | bytes 516104 | tf_op jit(solution)/shard_map/ppermute | solution.py:72
  203.8 53.7 %collective-permute-start.11 = (bf16[64,5376]{1,0:T(8,128)(2,1)S(1)}, bf16[64,5376]{1,0:T(8,128)(2,1)S(1)}, u32[]{:S(2)}, u32[]{:S(2)}) collective-permute-start(bf16[64,5376]{1,0:T(8,128)(2,1)S(1)} %get-tuple-element.54), channel_id=1, source_target_pairs={{0,1},{1,2},{2,3},{3,0},{4,5},{5,6},{6,7},{7,4},{8,9},{9,10},{10,1... | collective-permute-start | bytes 2064392 | tf_op jit(solution)/shard_map/ppermute | solution.py:53
  207.4 51.0 %collective-permute-start.12 = (bf16[64,5376]{1,0:T(8,128)(2,1)S(1)}, bf16[64,5376]{1,0:T(8,128)(2,1)S(1)}, u32[]{:S(2)}, u32[]{:S(2)}) collective-permute-start(bf16[64,5376]{1,0:T(8,128)(2,1)S(1)} %get-tuple-element.60), channel_id=1, source_target_pairs={{0,2},{1,3},{2,0},{3,1},{4,6},{5,7},{6,4},{7,5},{8,10},{9,11},{10,... | collective-permute-start | bytes 2064392 | tf_op jit(solution)/shard_map/ppermute | solution.py:53
  211.5 6.3 %collective-permute-start.19 = (bf16[2,168,256]{2,1,0:T(8,128)(2,1)S(1)}, bf16[2,168,256]{2,1,0:T(8,128)(2,1)S(1)}, u32[]{:S(2)}, u32[]{:S(2)}) collective-permute-start(bf16[2,168,256]{2,1,0:T(8,128)(2,1)S(1)} %fusion.57), channel_id=1, source_target_pairs={{0,32},{8,40},{16,48},{24,56},{32,64},{40,72},{48,80},{56,88},{64,... | collective-permute-start | bytes 516104 | tf_op jit(solution)/shard_map/ppermute | solution.py:72
  214.2 7.1 %collective-permute-start.27 = (bf16[2,168,256]{2,1,0:T(8,128)(2,1)S(1)}, bf16[2,168,256]{2,1,0:T(8,128)(2,1)S(1)}, u32[]{:S(2)}, u32[]{:S(2)}) collective-permute-start(bf16[2,168,256]{2,1,0:T(8,128)(2,1)S(1)} %fusion.40), channel_id=1, source_target_pairs={{0,224},{8,232},{16,240},{24,248},{32,0},{40,8},{48,16},{56,24},{6... | collective-permute-start | bytes 516104 | tf_op jit(solution)/shard_map/ppermute | solution.py:72
  217.8 6.4 %collective-permute-start.20 = (bf16[2,168,256]{2,1,0:T(8,128)(2,1)S(1)}, bf16[2,168,256]{2,1,0:T(8,128)(2,1)S(1)}, u32[]{:S(2)}, u32[]{:S(2)}) collective-permute-start(bf16[2,168,256]{2,1,0:T(8,128)(2,1)S(1)} %fusion.46), channel_id=1, source_target_pairs={{0,32},{8,40},{16,48},{24,56},{32,64},{40,72},{48,80},{56,88},{64,... | collective-permute-start | bytes 516104 | tf_op jit(solution)/shard_map/ppermute | solution.py:72
  221.3 6.9 %collective-permute-start.28 = (bf16[2,168,256]{2,1,0:T(8,128)(2,1)S(1)}, bf16[2,168,256]{2,1,0:T(8,128)(2,1)S(1)}, u32[]{:S(2)}, u32[]{:S(2)}) collective-permute-start(bf16[2,168,256]{2,1,0:T(8,128)(2,1)S(1)} %fusion.39), channel_id=1, source_target_pairs={{0,224},{8,232},{16,240},{24,248},{32,0},{40,8},{48,16},{56,24},{6... | collective-permute-start | bytes 516104 | tf_op jit(solution)/shard_map/ppermute | solution.py:72
  224.2 6.7 %collective-permute-start.21 = (bf16[2,168,256]{2,1,0:T(8,128)(2,1)S(1)}, bf16[2,168,256]{2,1,0:T(8,128)(2,1)S(1)}, u32[]{:S(2)}, u32[]{:S(2)}) collective-permute-start(bf16[2,168,256]{2,1,0:T(8,128)(2,1)S(1)} %fusion.45), channel_id=1, source_target_pairs={{0,32},{8,40},{16,48},{24,56},{32,64},{40,72},{48,80},{56,88},{64,... | collective-permute-start | bytes 516104 | tf_op jit(solution)/shard_map/ppermute | solution.py:72
  228.2 6.7 %collective-permute-start.29 = (bf16[2,168,256]{2,1,0:T(8,128)(2,1)S(1)}, bf16[2,168,256]{2,1,0:T(8,128)(2,1)S(1)}, u32[]{:S(2)}, u32[]{:S(2)}) collective-permute-start(bf16[2,168,256]{2,1,0:T(8,128)(2,1)S(1)} %fusion.38), channel_id=1, source_target_pairs={{0,224},{8,232},{16,240},{24,248},{32,0},{40,8},{48,16},{56,24},{6... | collective-permute-start | bytes 516104 | tf_op jit(solution)/shard_map/ppermute | solution.py:72
  230.9 6.7 %collective-permute-start.22 = (bf16[2,168,256]{2,1,0:T(8,128)(2,1)S(1)}, bf16[2,168,256]{2,1,0:T(8,128)(2,1)S(1)}, u32[]{:S(2)}, u32[]{:S(2)}) collective-permute-start(bf16[2,168,256]{2,1,0:T(8,128)(2,1)S(1)} %fusion.44), channel_id=1, source_target_pairs={{0,32},{8,40},{16,48},{24,56},{32,64},{40,72},{48,80},{56,88},{64,... | collective-permute-start | bytes 516104 | tf_op jit(solution)/shard_map/ppermute | solution.py:72
  234.9 7.0 %collective-permute-start.30 = (bf16[2,168,256]{2,1,0:T(8,128)(2,1)S(1)}, bf16[2,168,256]{2,1,0:T(8,128)(2,1)S(1)}, u32[]{:S(2)}, u32[]{:S(2)}) collective-permute-start(bf16[2,168,256]{2,1,0:T(8,128)(2,1)S(1)} %fusion.37), channel_id=1, source_target_pairs={{0,224},{8,232},{16,240},{24,248},{32,0},{40,8},{48,16},{56,24},{6... | collective-permute-start | bytes 516104 | tf_op jit(solution)/shard_map/ppermute | solution.py:72
  237.7 7.5 %collective-permute-start.23 = (bf16[2,168,256]{2,1,0:T(8,128)(2,1)S(1)}, bf16[2,168,256]{2,1,0:T(8,128)(2,1)S(1)}, u32[]{:S(2)}, u32[]{:S(2)}) collective-permute-start(bf16[2,168,256]{2,1,0:T(8,128)(2,1)S(1)} %fusion.43), channel_id=1, source_target_pairs={{0,32},{8,40},{16,48},{24,56},{32,64},{40,72},{48,80},{56,88},{64,... | collective-permute-start | bytes 516104 | tf_op jit(solution)/shard_map/ppermute | solution.py:72
  242.0 8.1 %collective-permute-start.31 = (bf16[2,168,256]{2,1,0:T(8,128)(2,1)S(1)}, bf16[2,168,256]{2,1,0:T(8,128)(2,1)S(1)}, u32[]{:S(2)}, u32[]{:S(2)}) collective-permute-start(bf16[2,168,256]{2,1,0:T(8,128)(2,1)S(1)} %fusion.36), channel_id=1, source_target_pairs={{0,224},{8,232},{16,240},{24,248},{32,0},{40,8},{48,16},{56,24},{6... | collective-permute-start | bytes 516104 | tf_op jit(solution)/shard_map/ppermute | solution.py:72
  245.3 8.4 %collective-permute-start.24 = (bf16[2,168,256]{2,1,0:T(8,128)(2,1)S(1)}, bf16[2,168,256]{2,1,0:T(8,128)(2,1)S(1)}, u32[]{:S(2)}, u32[]{:S(2)}) collective-permute-start(bf16[2,168,256]{2,1,0:T(8,128)(2,1)S(1)} %fusion.42), channel_id=1, source_target_pairs={{0,32},{8,40},{16,48},{24,56},{32,64},{40,72},{48,80},{56,88},{64,... | collective-permute-start | bytes 516104 | tf_op jit(solution)/shard_map/ppermute | solution.py:72
  250.1 12.4 %collective-permute-start.32 = (bf16[2,168,256]{2,1,0:T(8,128)(2,1)S(1)}, bf16[2,168,256]{2,1,0:T(8,128)(2,1)}, u32[]{:S(2)}, u32[]{:S(2)}) collective-permute-start(bf16[2,168,256]{2,1,0:T(8,128)(2,1)S(1)} %fusion.35), channel_id=1, source_target_pairs={{0,224},{8,232},{16,240},{24,248},{32,0},{40,8},{48,16},{56,24},{6... | collective-permute-start | bytes 516104 | tf_op jit(solution)/shard_map/ppermute | solution.py:72
  253.7 9.6 %collective-permute-start.25 = (bf16[2,168,256]{2,1,0:T(8,128)(2,1)S(1)}, bf16[2,168,256]{2,1,0:T(8,128)(2,1)}, u32[]{:S(2)}, u32[]{:S(2)}) collective-permute-start(bf16[2,168,256]{2,1,0:T(8,128)(2,1)S(1)} %fusion.41), channel_id=1, source_target_pairs={{0,32},{8,40},{16,48},{24,56},{32,64},{40,72},{48,80},{56,88},{64,... | collective-permute-start | bytes 516104 | tf_op jit(solution)/shard_map/ppermute | solution.py:72
  257.5 14.2 %collective-permute-start.13 = (bf16[64,5376]{1,0:T(8,128)(2,1)}, bf16[64,5376]{1,0:T(8,128)(2,1)S(1)}, u32[]{:S(2)}, u32[]{:S(2)}) collective-permute-start(bf16[64,5376]{1,0:T(8,128)(2,1)} %get-tuple-element.59), channel_id=1, source_target_pairs={{0,3},{1,0},{2,1},{3,2},{4,7},{5,4},{6,5},{7,6},{8,11},{9,8},{10,9... | collective-permute-start | bytes 2064392 | tf_op jit(solution)/shard_map/ppermute | solution.py:53
  257.5 20.1 %collective-permute-start.14 = (bf16[64,5376]{1,0:T(8,128)(2,1)}, bf16[64,5376]{1,0:T(8,128)(2,1)}, u32[]{:S(2)}, u32[]{:S(2)}) collective-permute-start(bf16[64,5376]{1,0:T(8,128)(2,1)} %get-tuple-element.58), channel_id=1, source_target_pairs={{0,4},{1,5},{2,6},{3,7},{4,0},{5,1},{6,2},{7,3},{8,12},{9,13},{10,... | collective-permute-start | bytes 2064392 | tf_op jit(solution)/shard_map/ppermute | solution.py:53
  258.4 34.6 %collective-permute-start.15 = (bf16[64,5376]{1,0:T(8,128)(2,1)}, bf16[64,5376]{1,0:T(8,128)(2,1)}, u32[]{:S(2)}, u32[]{:S(2)}) collective-permute-start(bf16[64,5376]{1,0:T(8,128)(2,1)} %get-tuple-element.57), channel_id=1, source_target_pairs={{0,5},{1,6},{2,7},{3,4},{4,1},{5,2},{6,3},{7,0},{8,13},{9,14},{10,... | collective-permute-start | bytes 2064392 | tf_op jit(solution)/shard_map/ppermute | solution.py:53
  262.5 46.3 %collective-permute-start.16 = (bf16[64,5376]{1,0:T(8,128)(2,1)}, bf16[64,5376]{1,0:T(8,128)(2,1)}, u32[]{:S(2)}, u32[]{:S(2)}) collective-permute-start(bf16[64,5376]{1,0:T(8,128)(2,1)} %get-tuple-element.56), channel_id=1, source_target_pairs={{0,6},{1,7},{2,4},{3,5},{4,2},{5,3},{6,0},{7,1},{8,14},{9,15},{10,... | collective-permute-start | bytes 2064392 | tf_op jit(solution)/shard_map/ppermute | solution.py:53
  263.3 52.7 %collective-permute-start.17 = (bf16[64,5376]{1,0:T(8,128)(2,1)}, bf16[64,5376]{1,0:T(8,128)(2,1)}, u32[]{:S(2)}, u32[]{:S(2)}) collective-permute-start(bf16[64,5376]{1,0:T(8,128)(2,1)} %get-tuple-element.55), channel_id=1, source_target_pairs={{0,7},{1,4},{2,5},{3,6},{4,3},{5,0},{6,1},{7,2},{8,15},{9,12},{10,... | collective-permute-start | bytes 2064392 | tf_op jit(solution)/shard_map/ppermute | solution.py:53
  271.7 47.7 %collective-permute-start.33 = (bf16[168,512]{1,0:T(8,128)(2,1)S(1)}, bf16[168,512]{1,0:T(8,128)(2,1)S(1)}, u32[]{:S(2)}, u32[]{:S(2)}) collective-permute-start(bf16[168,512]{1,0:T(8,128)(2,1)S(1)} %fusion.59), channel_id=1, source_target_pairs={{0,16},{8,24},{16,0},{24,8},{32,48},{40,56},{48,32},{56,40},{64,80... | collective-permute-start | bytes 516104 | tf_op jit(solution)/shard_map/ppermute | solution.py:83
  (4 other events, 6.1 us)

commit v3 on v2

--- a/solution.py
+++ b/solution.py
@@ -94,6 +94,20 @@
     down = ring_scatter_sum(grid[..., half:], axis, outer, middle * inner, False)
     grid = jnp.concatenate([up, down], axis=-1)
     return pair_scatter_sum(grid, axis, inner)
+
+
+def gather_all(block, axis):
+    size = lax.axis_size(axis)
+    copies = jnp.broadcast_to(block[None], (size,) + block.shape)
+    received = lax.all_to_all(copies, axis, 0, 0)
+    return received.reshape((size * block.shape[0],) + block.shape[1:])
+
+
+def exchange_sum(full, axis):
+    size = lax.axis_size(axis)
+    pieces = full.reshape((size, full.shape[0] // size) + full.shape[1:])
+    received = lax.all_to_all(pieces, axis, 0, 0)
+    return jnp.sum(received.astype(jnp.float32), axis=0)
 
 
 def rope_tables(positions, head_size):
@@ -199,7 +213,7 @@
     window_rows = block_rows + WINDOW
     reach_blocks = (WINDOW - 2) // token_count + 1
     position_base = lax.axis_index("ctx") * token_count
-    gathered = gather_over(hidden, "heads")
+    gathered = gather_all(hidden, "heads")
     query_proj = jnp.dot(gathered, query_weight, preferred_element_type=jnp.float32)
     key_proj = jnp.dot(gathered, key_weight, preferred_element_type=jnp.float32)
     value_proj = jnp.dot(gathered, value_weight, preferred_element_type=jnp.float32)
@@ -288,7 +302,7 @@
     partial_sum = partial_sum + lax.dot_general(
         grad_key, key_weight, back_contract, preferred_element_type=jnp.float32
     )
-    input_grad = scatter_sum_over(
+    input_grad = exchange_sum(
         (
             partial_sum
             + lax.dot_general(

time: 325 us -> 275 us (0.85)
  starting transfers between devices: 120 us -> 50.2 us
  waiting for transfers between devices: 84.6 us -> 101 us
  local copies, waits for them, and re-layouts: 44 us -> 36.4 us
  matrix products: 47.8 us -> 53.9 us
  other arithmetic: 23.2 us -> 26.8 us
    ppermute x14 -> x0, starting transfers between devices: 65.1 us -> none  [the longest x7 47.2 us: gather_over(): lax.ppermute(block, axis, route)]
    all_to_all x0 -> x2, waiting for transfers between devices: none -> 54.9 us  [the longest x1 54.8 us: gather_all(): received = lax.all_to_all(copies, axis, 0, 0)]
    ppermute x14 -> x0, waiting for transfers between devices: 50.7 us -> none  [the longest x7 42.3 us: scatter_sum_over(): total = total + lax.ppermute(piece, axis, route).astype(jnp.float32)]
    unnamed x77 -> x40, local copies, waits for them, and re-layouts: 23.6 us -> 4.59 us
    ppermute x4, starting transfers between devices: 24.8 us -> 9.92 us  [passed_along(): return lax.ppermute(block, axis, route)]
    mul x0 -> x1, local copies, waits for them, and re-layouts: none -> 12.1 us  [per_device(): lax.dot_general(gathered, jnp.concatenate([grad_query, grad_key, grad_val...]
    all_to_all x0 -> x2, starting transfers between devices: none -> 11.8 us  [the longest x1 7.06 us: gather_all(): received = lax.all_to_all(copies, axis, 0, 0)]
    convert_element_type x12, other arithmetic: 0.63 us -> 8.38 us  [ring_scatter_sum(): running.astype(jnp.bfloat16)]
  transfers between devices with their start and end apart: 34 -> 22, of which waited for: 18 -> 14; matrix products, arithmetic and copies ran while one was open for 19% -> 18% of each run, Pallas kernels for 0% -> 0%
where the time goes in v3:
time: 275 us; the launch traced here: 270 us
  waiting for transfers between devices  101 us (37%)
  matrix products  53.9 us (20%)
  starting transfers between devices  50.2 us (18%)
  local copies, waits for them, and re-layouts  36.4 us (13%)
  other arithmetic  26.8 us (10%)
    all_to_all x1, waiting for transfers between devices, gather_all(): received = lax.all_to_all(copies, axis, 0, 0)  54.8 us
    ppermute x14, starting transfers between devices, ring_scatter_sum(): lax.ppermute(running.astype(jnp.bfloat16), axis, route).astype(jnp.float32)  27.9 us
    ppermute x4, waiting for transfers between devices, passed_along(): return lax.ppermute(block, axis, route)  21.1 us
    ppermute x14, waiting for transfers between devices, ring_scatter_sum(): lax.ppermute(running.astype(jnp.bfloat16), axis, route).astype(jnp.float32)  20.8 us
    mul x1, local copies, waits for them, and re-layouts, per_device(): lax.dot_general(gathered, jnp.concatenate([grad_query, grad_key, grad_val...  12.1 us
    ppermute x4, starting transfers between devices, passed_along(): return lax.ppermute(block, axis, route)  9.92 us
    dot_general x1, matrix products, per_device(): lax.dot_general(grad_value, value_weight, back_contract, preferred_elemen...  8.63 us
    dot_general x1, matrix products, per_device(): lax.dot_general(gathered, jnp.concatenate([grad_query, grad_key, grad_val...  8.61 us
  transfers between devices with their start and end apart: 22, of which 14 were waited for; matrix products, arithmetic and copies ran while one was open for 18% of the time, Pallas kernels for 0%

profile of v3, /device:TPU:96, one launch (start us, length us, event | category | flops | bytes accessed | tf_op | source)
XLA Modules:
  0.0 269.9 jit_solution(2705016271085171141)
XLA Ops:
  0.6 4.0 %broadcast_in_dim.71 = bf16[8,64,5376]{2,1,0:T(8,128)(2,1)} broadcast(bf16[64,5376]{1,0:T(8,128)(2,1)} %param.7), dimensions={1,2} | broadcast | bytes 6193152 | tf_op jit(solution)/shard_map/broadcast_in_dim | solution.py:101
  4.6 7.1 %all-to-all-start = ((bf16[8,64,5376]{2,1,0:T(8,128)(2,1)}), bf16[8,64,5376]{2,1,0:T(8,128)(2,1)}, u32[]{:S(2)}, u32[]{:S(2)}) async-start(bf16[8,64,5376]{2,1,0:T(8,128)(2,1)} %broadcast_in_dim.71), calls=%async_computation | async-start | bytes 11010048 | tf_op jit(solution)/shard_map/all_to_all | solution.py:102
  11.8 0.9 copy.36
  12.7 4.7 %copy.55 = bf16[256,5376]{1,0:T(8,128)(2,1)} copy(bf16[256,5376]{0,1:T(8,128)(2,1)} %bitcast.209) | data formatting | bytes 5505024 | tf_op jit(solution)/shard_map/dot_general | solution.py:217
  17.4 1.2 multiply_cosine_fusion
  18.7 1.2 fusion.7
  19.9 54.8 %all-to-all-done = bf16[8,64,5376]{2,1,0:T(8,128)(2,1)} async-done(((bf16[8,64,5376]{2,1,0:T(8,128)(2,1)}), bf16[8,64,5376]{2,1,0:T(8,128)(2,1)}, u32[]{:S(2)}, u32[]{:S(2)}) %all-to-all-start) | async-done | bytes 5505056 | tf_op jit(solution)/shard_map/all_to_all | solution.py:102
  74.7 4.5 %fusion.10 = bf16[1,512,128]{1,2,0:T(8,128)(2,1)S(1)} fusion(bf16[512,5376]{1,0:T(8,128)(2,1)} %bitcast.2, bf16[5376,128]{1,0:T(8,128)(2,1)S(1)} %copy-done.4), kind=kOutput, calls=%fused_computation.29 | convolution fusion | flops 704708608 | bytes 7012352 | tf_op jit(solution)/shard_map/dot_general | solution.py:219
  79.3 4.7 %multiply_reduce_fusion.3 = (f32[512]{0:T(512)S(1)}, f32[512,128]{0,1:T(8,128)S(1)}) fusion(bf16[512,5376]{1,0:T(8,128)(2,1)} %bitcast.2, bf16[5376,128]{1,0:T(8,128)(2,1)S(1)} %copy-done), kind=kOutput, calls=%fused_computation.104 | convolution fusion | flops 704773632 | bytes 7145472 | tf_op jit(solution)/shard_map/dot_general | solution.py:218
  84.7 1.9 collective-permute-start.1
  86.6 2.7 collective-permute-start
  89.3 4.2 %multiply_reduce_fusion.2 = (f32[512,2]{0,1:T(2,128)S(1)}, f32[512,2,128]{0,2,1:T(8,128)S(1)}) fusion(bf16[512,5376,1]{1,0,2:T(8,128)(2,1)} %bitcast.10, bf16[2,128,5376]{2,1,0:T(8,128)(2,1)S(1)} %bitcast.210), kind=kOutput, calls=%fused_computation.53 | convolution fusion | flops 1409547264 | bytes 8785920 | tf_op jit(solution)/shard_map/dot_general | solution.py:217
  93.8 4.8 %collective-permute-done = bf16[2,512,128]{1,2,0:T(8,128)(2,1)S(1)} collective-permute-done((bf16[2,512,128]{1,2,0:T(8,128)(2,1)S(1)}, bf16[2,512,128]{1,2,0:T(8,128)(2,1)S(1)}, u32[]{:S(2)}, u32[]{:S(2)}) %collective-permute-start) | collective-permute-done | bytes 262176 | tf_op jit(solution)/shard_map/ppermute | solution.py:18
  98.6 1.3 fusion.2
  99.9 1.3 exponential_reduce_fusion
  101.3 2.9 %bitcast_convert_fusion = (f32[2,512,128]{1,2,0:T(8,128)}, bf16[128,2,512]{2,0,1:T(8,128)(2,1)}) fusion(f32[1536,512,2]{1,0,2:T(8,128)S(1)} %get-tuple-element.89, f32[2,512]{1,0:T(2,128)S(1)} %log_add_fusion, pred[512,1536]{0,1:T(8,128)(4,1)S(1)} %fusion.7, bf16[2,1536,128]{1,2,0:T(8,128)(2,1)S(1)} %maximum_maximum_fusion), kind=kOutput, calls=%fused_computation.97 | convolution fusion | flops 409206784 | bytes 8261632 | tf_op jit(solution)/shard_map/while/body/eval_jaxpr/kgqj,jkd->qkgd/dot_general | solution.py:160
  104.1 3.0 %convolution_bitcast_fusion = f32[1,1536,128]{1,2,0:T(8,128)} fusion(bf16[512,2,128]{0,2,1:T(8,128)(2,1)S(1)} %copy-done.16, f32[1536,512,2]{1,0,2:T(8,128)S(1)} %get-tuple-element.89, f32[2,512]{1,0:T(2,128)S(1)} %log_add_fusion, pred[512,1536]{0,1:T(8,128)(4,1)S(1)} %fusion.7), kind=kOutput, calls=%fused_computation.19 | convolution fusion | flops 408944640 | bytes 8130560 | tf_op jit(solution)/shard_map/while/body/eval_jaxpr/kgqj,qkgd->jkd/dot_general | solution.py:199
  107.2 2.1 copy.49
  109.2 2.4 multiply_reduce_fusion
  111.7 1.1 copy.50
  112.7 5.3 %fusion.4 = bf16[2,512,1536]{1,2,0:T(8,128)(2,1)S(1)} fusion(bf16[512,2,128]{0,2,1:T(8,128)(2,1)} %copy.36, f32[1536,512,2]{1,0,2:T(8,128)} %copy-done.1, f32[2,512]{1,0:T(2,128)S(1)} %copy.50, f32[2,512]{1,0:T(2,128)S(1)} %log_add_fusion, pred[512,1536]{0,1:T(8,128)(4,1)S(1)} %fusion.7, bf16[2,1536,128]{1,2,0:T(8,128)(2,1)} %copy-done.5), kind=kOutput, calls=%fused_computation.14 | convolution fusion | flops 412090368 | bytes 10887168 | tf_op jit(solution)/shard_map/while/body/eval_jaxpr/qkgd,jkd->kgqj/dot_general | solution.py:189
  118.7 1.2 convolution_bitcast_fusion.1
  120.1 1.9 collective-permute-start.2
  122.0 3.4 %collective-permute-start.3 = (f32[2,512,128]{1,2,0:T(8,128)S(1)}, f32[2,512,128]{1,2,0:T(8,128)S(1)}, u32[]{:S(2)}, u32[]{:S(2)}) collective-permute-start(f32[2,512,128]{1,2,0:T(8,128)S(1)} %get-tuple-element.60), channel_id=1, source_target_pairs={{16,0},{24,8},{32,16},{40,24},{48,32},{56,40},{64,48},{72,56},{80,... | collective-permute-start | bytes 1572872 | tf_op jit(solution)/shard_map/ppermute | solution.py:18
  125.7 6.8 %collective-permute-done.2 = f32[2,512,128]{1,2,0:T(8,128)S(1)} collective-permute-done((f32[2,512,128]{1,2,0:T(8,128)S(1)}, f32[2,512,128]{1,2,0:T(8,128)S(1)}, u32[]{:S(2)}, u32[]{:S(2)}) %collective-permute-start.2) | collective-permute-done | bytes 524320 | tf_op jit(solution)/shard_map/ppermute | solution.py:18
  132.5 9.6 %collective-permute-done.3 = f32[2,512,128]{1,2,0:T(8,128)S(1)} collective-permute-done((f32[2,512,128]{1,2,0:T(8,128)S(1)}, f32[2,512,128]{1,2,0:T(8,128)S(1)}, u32[]{:S(2)}, u32[]{:S(2)}) %collective-permute-start.3) | collective-permute-done | bytes 524320 | tf_op jit(solution)/shard_map/ppermute | solution.py:18
  143.1 8.6 %multiply_bitcast_fusion = f32[5376,512]{0,1:T(8,128)} fusion(bf16[512,5376]{1,0:T(8,128)(2,1)} %bitcast.2, bf16[512,128]{0,1:T(8,128)(2,1)S(1)} %fusion.59, bf16[512,128]{0,1:T(8,128)(2,1)S(1)} %fusion.60, bf16[512,256]{0,1:T(8,128)(2,1)S(1)} %bitcast.211), kind=kOutput, calls=%fused_computation | convolution fusion | flops 2822897664 | bytes 17039360 | tf_op jit(solution)/shard_map/dot_general | solution.py:285
  151.7 12.1 %copy.37 = f32[5376,512]{1,0:T(8,128)} copy(f32[5376,512]{0,1:T(8,128)} %multiply_bitcast_fusion) | data formatting | bytes 22020096 | tf_op jit(solution)/shard_map/mul | solution.py:285
  163.8 4.5 %fusion.8 = bf16[8,2,168,512]{3,2,1,0:T(8,128)(2,1)} fusion(f32[8,2,2,168,512]{4,3,2,1,0:T(8,128)} %bitcast.206, s32[]{:T(128)S(6)} %select_n.172), kind=kLoop, calls=%fused_computation.18 | loop fusion | bytes 5505028 | tf_op jit(solution)/shard_map/convert_element_type | solution.py:83
  168.3 7.5 %fusion.76 = f32[512,5376]{1,0:T(8,128)} fusion(bf16[512,256]{0,1:T(8,128)(2,1)S(1)} %bitcast.212, bf16[5376,256]{1,0:T(8,128)(2,1)} %param.8), kind=kOutput, calls=%fused_computation.148 | convolution fusion | flops 1409286144 | bytes 14024704 | tf_op jit(solution)/shard_map/dot_general | solution.py:299
  175.8 1.6 fusion.77
  177.4 8.6 %add_convert_fusion = bf16[512,5376]{1,0:T(8,128)(2,1)} fusion(f32[512,5376]{1,0:T(8,128)} %fusion.76, f32[512,5376]{1,0:T(8,128)S(1)} %fusion.77, bf16[5376,128]{1,0:T(8,128)(2,1)} %param.10, f32[2,512,128]{1,2,0:T(8,128)S(1)} %fusion.15), kind=kOutput, calls=%fused_computation.1 | convolution fusion | flops 712900608 | bytes 29032448 | tf_op jit(solution)/shard_map/dot_general | solution.py:308
  186.1 4.8 %all-to-all-start.1 = ((bf16[8,64,5376]{2,1,0:T(8,128)(2,1)}), bf16[8,64,5376]{2,1,0:T(8,128)(2,1)}, u32[]{:S(2)}, u32[]{:S(2)}) async-start(bf16[8,64,5376]{2,1,0:T(8,128)(2,1)} %bitcast.208), calls=%async_computation.1 | async-start | bytes 11010048 | tf_op jit(solution)/shard_map/all_to_all | solution.py:109
  190.8 4.4 %bitcast_add_fusion = f32[8,2,168,512]{3,2,1,0:T(8,128)S(1)} fusion(bf16[8,2,168,512]{3,2,1,0:T(8,128)(2,1)} %collective-permute-done.4, f32[8,2,2,168,512]{4,3,2,1,0:T(8,128)} %bitcast.207, s32[]{:T(128)S(6)} %select_n.171), kind=kLoop, calls=%fused_computation.9 | loop fusion | flops 2752512 | bytes 13762564 | tf_op jit(solution)/shard_map/add | solution.py:83
  195.2 2.0 fusion.73
  197.2 1.6 copy-done.3
  198.8 4.4 %collective-permute-start.5 = (bf16[2,168,256]{2,1,0:T(8,128)(2,1)S(1)}, bf16[2,168,256]{2,1,0:T(8,128)(2,1)S(1)}, u32[]{:S(2)}, u32[]{:S(2)}) collective-permute-start(bf16[2,168,256]{2,1,0:T(8,128)(2,1)S(1)} %fusion.50), channel_id=1, source_target_pairs={{0,32},{8,40},{16,48},{24,56},{32,64},{40,72},{48,80},{56,88},{64,... | collective-permute-start | bytes 516104 | tf_op jit(solution)/shard_map/ppermute | solution.py:72
  203.2 1.1 fusion.51
  204.7 2.7 %collective-permute-done.5 = bf16[2,168,256]{2,1,0:T(8,128)(2,1)S(1)} collective-permute-done((bf16[2,168,256]{2,1,0:T(8,128)(2,1)S(1)}, bf16[2,168,256]{2,1,0:T(8,128)(2,1)S(1)}, u32[]{:S(2)}, u32[]{:S(2)}) %collective-permute-start.5) | collective-permute-done | bytes 172064 | tf_op jit(solution)/shard_map/ppermute | solution.py:72
  207.4 1.0 fusion.39
  208.5 3.8 %collective-permute-start.6 = (bf16[2,168,256]{2,1,0:T(8,128)(2,1)S(1)}, bf16[2,168,256]{2,1,0:T(8,128)(2,1)S(1)}, u32[]{:S(2)}, u32[]{:S(2)}) collective-permute-start(bf16[2,168,256]{2,1,0:T(8,128)(2,1)S(1)} %fusion.39), channel_id=1, source_target_pairs={{0,32},{8,40},{16,48},{24,56},{32,64},{40,72},{48,80},{56,88},{64,... | collective-permute-start | bytes 516104 | tf_op jit(solution)/shard_map/ppermute | solution.py:72
  212.3 1.0 fusion.33
  213.4 2.3 collective-permute-done.6
  215.7 1.0 fusion.38
  216.7 3.8 %collective-permute-start.7 = (bf16[2,168,256]{2,1,0:T(8,128)(2,1)S(1)}, bf16[2,168,256]{2,1,0:T(8,128)(2,1)S(1)}, u32[]{:S(2)}, u32[]{:S(2)}) collective-permute-start(bf16[2,168,256]{2,1,0:T(8,128)(2,1)S(1)} %fusion.38), channel_id=1, source_target_pairs={{0,32},{8,40},{16,48},{24,56},{32,64},{40,72},{48,80},{56,88},{64,... | collective-permute-start | bytes 516104 | tf_op jit(solution)/shard_map/ppermute | solution.py:72
  220.5 1.0 fusion.32
  221.6 1.8 collective-permute-done.7
  223.4 1.0 fusion.37
  224.4 3.8 %collective-permute-start.8 = (bf16[2,168,256]{2,1,0:T(8,128)(2,1)S(1)}, bf16[2,168,256]{2,1,0:T(8,128)(2,1)S(1)}, u32[]{:S(2)}, u32[]{:S(2)}) collective-permute-start(bf16[2,168,256]{2,1,0:T(8,128)(2,1)S(1)} %fusion.37), channel_id=1, source_target_pairs={{0,32},{8,40},{16,48},{24,56},{32,64},{40,72},{48,80},{56,88},{64,... | collective-permute-start | bytes 516104 | tf_op jit(solution)/shard_map/ppermute | solution.py:72
  228.4 2.8 %collective-permute-done.8 = bf16[2,168,256]{2,1,0:T(8,128)(2,1)S(1)} collective-permute-done((bf16[2,168,256]{2,1,0:T(8,128)(2,1)S(1)}, bf16[2,168,256]{2,1,0:T(8,128)(2,1)S(1)}, u32[]{:S(2)}, u32[]{:S(2)}) %collective-permute-start.8) | collective-permute-done | bytes 172064 | tf_op jit(solution)/shard_map/ppermute | solution.py:72
  231.1 1.0 fusion.36
  232.2 3.8 %collective-permute-start.9 = (bf16[2,168,256]{2,1,0:T(8,128)(2,1)S(1)}, bf16[2,168,256]{2,1,0:T(8,128)(2,1)S(1)}, u32[]{:S(2)}, u32[]{:S(2)}) collective-permute-start(bf16[2,168,256]{2,1,0:T(8,128)(2,1)S(1)} %fusion.36), channel_id=1, source_target_pairs={{0,32},{8,40},{16,48},{24,56},{32,64},{40,72},{48,80},{56,88},{64,... | collective-permute-start | bytes 516104 | tf_op jit(solution)/shard_map/ppermute | solution.py:72
  236.1 2.8 %collective-permute-done.9 = bf16[2,168,256]{2,1,0:T(8,128)(2,1)S(1)} collective-permute-done((bf16[2,168,256]{2,1,0:T(8,128)(2,1)S(1)}, bf16[2,168,256]{2,1,0:T(8,128)(2,1)S(1)}, u32[]{:S(2)}, u32[]{:S(2)}) %collective-permute-start.9) | collective-permute-done | bytes 172064 | tf_op jit(solution)/shard_map/ppermute | solution.py:72
  238.9 1.0 fusion.35
  239.9 3.8 %collective-permute-start.10 = (bf16[2,168,256]{2,1,0:T(8,128)(2,1)S(1)}, bf16[2,168,256]{2,1,0:T(8,128)(2,1)S(1)}, u32[]{:S(2)}, u32[]{:S(2)}) collective-permute-start(bf16[2,168,256]{2,1,0:T(8,128)(2,1)S(1)} %fusion.35), channel_id=1, source_target_pairs={{0,32},{8,40},{16,48},{24,56},{32,64},{40,72},{48,80},{56,88},{64,... | collective-permute-start | bytes 516104 | tf_op jit(solution)/shard_map/ppermute | solution.py:72
  243.8 2.8 %collective-permute-done.10 = bf16[2,168,256]{2,1,0:T(8,128)(2,1)S(1)} collective-permute-done((bf16[2,168,256]{2,1,0:T(8,128)(2,1)S(1)}, bf16[2,168,256]{2,1,0:T(8,128)(2,1)S(1)}, u32[]{:S(2)}, u32[]{:S(2)}) %collective-permute-start.10) | collective-permute-done | bytes 172064 | tf_op jit(solution)/shard_map/ppermute | solution.py:72
  246.6 1.0 fusion.34
  247.6 3.8 %collective-permute-start.11 = (bf16[2,168,256]{2,1,0:T(8,128)(2,1)S(1)}, bf16[2,168,256]{2,1,0:T(8,128)(2,1)S(1)}, u32[]{:S(2)}, u32[]{:S(2)}) collective-permute-start(bf16[2,168,256]{2,1,0:T(8,128)(2,1)S(1)} %fusion.34), channel_id=1, source_target_pairs={{0,32},{8,40},{16,48},{24,56},{32,64},{40,72},{48,80},{56,88},{64,... | collective-permute-start | bytes 516104 | tf_op jit(solution)/shard_map/ppermute | solution.py:72
  251.5 2.8 %collective-permute-done.11 = bf16[2,168,256]{2,1,0:T(8,128)(2,1)S(1)} collective-permute-done((bf16[2,168,256]{2,1,0:T(8,128)(2,1)S(1)}, bf16[2,168,256]{2,1,0:T(8,128)(2,1)S(1)}, u32[]{:S(2)}, u32[]{:S(2)}) %collective-permute-start.11) | collective-permute-done | bytes 172064 | tf_op jit(solution)/shard_map/ppermute | solution.py:72
  254.3 1.0 bitcast_add_fusion.8
  255.3 2.8 %collective-permute-done.18 = bf16[2,168,256]{2,1,0:T(8,128)(2,1)S(1)} collective-permute-done((bf16[2,168,256]{2,1,0:T(8,128)(2,1)S(1)}, bf16[2,168,256]{2,1,0:T(8,128)(2,1)S(1)}, u32[]{:S(2)}, u32[]{:S(2)}) %collective-permute-start.18) | collective-permute-done | bytes 172064 | tf_op jit(solution)/shard_map/ppermute | solution.py:72
  258.8 0.8 copy.38
  259.6 4.1 %collective-permute-done.19 = bf16[168,512]{1,0:T(8,128)(2,1)S(1)} collective-permute-done((bf16[168,512]{1,0:T(8,128)(2,1)S(1)}, bf16[168,512]{1,0:T(8,128)(2,1)S(1)}, u32[]{:S(2)}, u32[]{:S(2)}) %collective-permute-start.19) | collective-permute-done | bytes 172064 | tf_op jit(solution)/shard_map/ppermute | solution.py:83
  265.1 4.4 %reduce_sum.71 = bf16[64,5376]{1,0:T(8,128)(2,1)} reduce(bf16[8,64,5376]{2,1,0:T(8,128)(2,1)} %all-to-all-done.1, bf16[]{:T(256)} %constant.276.clone.1), dimensions={0}, to_apply=%region_6.7 | reduce | flops 2408448 | bytes 6193154 | tf_op jit(solution)/shard_map/reduce_sum | solution.py:110
  (94 shorter events, 6.4 us)
Async XLA Ops:
  0.6 78.6 %copy-start = (bf16[5376,128]{1,0:T(8,128)(2,1)S(1)}, bf16[5376,128]{1,0:T(8,128)(2,1)}, u32[]{:S(2)}) copy-start(bf16[5376,128]{1,0:T(8,128)(2,1)} %param.9) | copy-start | bytes 4128772
  4.6 7.1 %copy-start.14 = (bf16[512,256]{1,0:T(8,128)(2,1)S(1)}, bf16[512,256]{1,0:T(8,128)(2,1)}, u32[]{:S(2)}) copy-start(bf16[512,256]{1,0:T(8,128)(2,1)} %param.13) | copy-start | bytes 786436
  4.6 70.1 %all-to-all-start = ((bf16[8,64,5376]{2,1,0:T(8,128)(2,1)}), bf16[8,64,5376]{2,1,0:T(8,128)(2,1)}, u32[]{:S(2)}, u32[]{:S(2)}) async-start(bf16[8,64,5376]{2,1,0:T(8,128)(2,1)} %broadcast_in_dim.71), calls=%async_computation | async-start | bytes 11010048 | tf_op jit(solution)/shard_map/all_to_all | solution.py:102
  11.8 5.7 %copy-start.9 = (bf16[512,2,128]{2,1,0:T(2,128)(2,1)}, bf16[512,2,128]{2,1,0:T(2,128)(2,1)S(1)}, u32[]{:S(2)}) copy-start(bf16[512,2,128]{2,1,0:T(2,128)(2,1)S(1)} %reshape.339) | copy-start | bytes 786436
  12.7 62.1 %copy-start.4 = (bf16[5376,128]{1,0:T(8,128)(2,1)S(1)}, bf16[5376,128]{1,0:T(8,128)(2,1)}, u32[]{:S(2)}) copy-start(bf16[5376,128]{1,0:T(8,128)(2,1)} %param.10) | copy-start | bytes 4128772
  79.2 4.7 %copy-start.18 = (f32[128]{0:T(128)S(1)}, f32[128]{0:T(128)}, u32[]{:S(2)}) copy-start(f32[128]{0:T(128)} %param.12) | copy-start | bytes 1540
  79.3 10.0 %copy-start.8 = (bf16[256,5376]{1,0:T(8,128)(2,1)S(1)}, bf16[256,5376]{1,0:T(8,128)(2,1)}, u32[]{:S(2)}) copy-start(bf16[256,5376]{1,0:T(8,128)(2,1)} %copy.55) | copy-start | bytes 8257540
  84.7 9.1 %collective-permute-start.1 = (bf16[2,512,128]{1,2,0:T(8,128)(2,1)S(1)}, bf16[2,512,128]{1,2,0:T(8,128)(2,1)S(1)}, u32[]{:S(2)}, u32[]{:S(2)}) collective-permute-start(bf16[2,512,128]{1,2,0:T(8,128)(2,1)S(1)} %pad_maximum_fusion.1), channel_id=1, source_target_pairs={{0,8},{8,16},{16,24},{24,32},{32,40},{40,48},{48,56},{56,64},{64,7... | collective-permute-start | bytes 786440 | tf_op jit(solution)/shard_map/ppermute | solution.py:18
  86.6 12.0 %collective-permute-start = (bf16[2,512,128]{1,2,0:T(8,128)(2,1)S(1)}, bf16[2,512,128]{1,2,0:T(8,128)(2,1)S(1)}, u32[]{:S(2)}, u32[]{:S(2)}) collective-permute-start(bf16[2,512,128]{1,2,0:T(8,128)(2,1)S(1)} %pad_maximum_fusion.1), channel_id=1, source_target_pairs={{0,16},{8,24},{16,32},{24,40},{32,48},{40,56},{48,64},{56,72},{64,... | collective-permute-start | bytes 786440 | tf_op jit(solution)/shard_map/ppermute | solution.py:18
  89.3 4.3 %copy-start.17 = (f32[128]{0:T(128)S(1)}, f32[128]{0:T(128)}, u32[]{:S(2)}) copy-start(f32[128]{0:T(128)} %param.11) | copy-start | bytes 1540
  89.3 4.4 %copy-start.10 = (f32[512,64]{0,1:T(8,128)S(1)}, f32[512,64]{0,1:T(8,128)}, u32[]{:S(2)}) copy-start(f32[512,64]{0,1:T(8,128)} %get-tuple-element.82) | copy-start | bytes 393220
  89.3 4.4 %copy-start.12 = (f32[512,64]{0,1:T(8,128)S(1)}, f32[512,64]{0,1:T(8,128)}, u32[]{:S(2)}) copy-start(f32[512,64]{0,1:T(8,128)} %get-tuple-element.83) | copy-start | bytes 393220
  98.6 2.6 copy-start.5
  99.9 4.2 %copy-start.1 = (f32[1536,512,2]{1,0,2:T(8,128)}, f32[1536,512,2]{1,0,2:T(8,128)S(1)}, u32[]{:S(2)}) copy-start(f32[1536,512,2]{1,0,2:T(8,128)S(1)} %get-tuple-element.89) | copy-start | bytes 18874372
  101.3 2.9 %copy-start.16 = (bf16[512,2,128]{0,2,1:T(8,128)(2,1)S(1)}, bf16[512,2,128]{0,2,1:T(8,128)(2,1)}, u32[]{:S(2)}) copy-start(bf16[512,2,128]{0,2,1:T(8,128)(2,1)} %copy.36) | copy-start | bytes 786436
  112.7 5.3 %copy-start.6 = (bf16[2,1536,128]{1,2,0:T(8,128)(2,1)S(1)}, bf16[2,1536,128]{1,2,0:T(8,128)(2,1)}, u32[]{:S(2)}) copy-start(bf16[2,1536,128]{1,2,0:T(8,128)(2,1)} %copy-done.5) | copy-start | bytes 2359300
  118.7 1.2 copy-start.11
  118.7 1.2 copy-start.13
  118.7 1.3 copy-start.7
  120.1 12.5 %collective-permute-start.2 = (f32[2,512,128]{1,2,0:T(8,128)S(1)}, f32[2,512,128]{1,2,0:T(8,128)S(1)}, u32[]{:S(2)}, u32[]{:S(2)}) collective-permute-start(f32[2,512,128]{1,2,0:T(8,128)S(1)} %get-tuple-element.59), channel_id=1, source_target_pairs={{8,0},{16,8},{24,16},{32,24},{40,32},{48,40},{56,48},{64,56},{72,6... | collective-permute-start | bytes 1572872 | tf_op jit(solution)/shard_map/ppermute | solution.py:18
  122.0 20.1 %collective-permute-start.3 = (f32[2,512,128]{1,2,0:T(8,128)S(1)}, f32[2,512,128]{1,2,0:T(8,128)S(1)}, u32[]{:S(2)}, u32[]{:S(2)}) collective-permute-start(f32[2,512,128]{1,2,0:T(8,128)S(1)} %get-tuple-element.60), channel_id=1, source_target_pairs={{16,0},{24,8},{32,16},{40,24},{48,32},{56,40},{64,48},{72,56},{80,... | collective-permute-start | bytes 1572872 | tf_op jit(solution)/shard_map/ppermute | solution.py:18
  168.3 22.5 %collective-permute-start.4 = (bf16[8,2,168,512]{3,2,1,0:T(8,128)(2,1)}, bf16[8,2,168,512]{3,2,1,0:T(8,128)(2,1)}, u32[]{:S(2)}, u32[]{:S(2)}) collective-permute-start(bf16[8,2,168,512]{3,2,1,0:T(8,128)(2,1)} %fusion.8), channel_id=1, source_target_pairs={{0,8},{8,0},{16,24},{24,16},{32,40},{40,32},{48,56},{56,48},{64,72... | collective-permute-start | bytes 8257544 | tf_op jit(solution)/shard_map/ppermute | solution.py:83
  186.1 79.1 %all-to-all-start.1 = ((bf16[8,64,5376]{2,1,0:T(8,128)(2,1)}), bf16[8,64,5376]{2,1,0:T(8,128)(2,1)}, u32[]{:S(2)}, u32[]{:S(2)}) async-start(bf16[8,64,5376]{2,1,0:T(8,128)(2,1)} %bitcast.208), calls=%async_computation.1 | async-start | bytes 11010048 | tf_op jit(solution)/shard_map/all_to_all | solution.py:109
  197.2 1.6 copy-start.3
  198.8 8.7 %collective-permute-start.5 = (bf16[2,168,256]{2,1,0:T(8,128)(2,1)S(1)}, bf16[2,168,256]{2,1,0:T(8,128)(2,1)S(1)}, u32[]{:S(2)}, u32[]{:S(2)}) collective-permute-start(bf16[2,168,256]{2,1,0:T(8,128)(2,1)S(1)} %fusion.50), channel_id=1, source_target_pairs={{0,32},{8,40},{16,48},{24,56},{32,64},{40,72},{48,80},{56,88},{64,... | collective-permute-start | bytes 516104 | tf_op jit(solution)/shard_map/ppermute | solution.py:72
  203.2 25.0 %copy-start.2 = (f32[8,2,168,256]{3,2,1,0:T(8,128)S(1)}, f32[8,2,168,256]{3,2,1,0:T(8,128)}, u32[]{:S(2)}) copy-start(f32[8,2,168,256]{3,2,1,0:T(8,128)} %get-tuple-element.57) | copy-start | bytes 8257540
  204.4 8.0 %collective-permute-start.12 = (bf16[2,168,256]{2,1,0:T(8,128)(2,1)S(1)}, bf16[2,168,256]{2,1,0:T(8,128)(2,1)S(1)}, u32[]{:S(2)}, u32[]{:S(2)}) collective-permute-start(bf16[2,168,256]{2,1,0:T(8,128)(2,1)S(1)} %fusion.51), channel_id=1, source_target_pairs={{0,224},{8,232},{16,240},{24,248},{32,0},{40,8},{48,16},{56,24},{6... | collective-permute-start | bytes 516104 | tf_op jit(solution)/shard_map/ppermute | solution.py:72
  208.5 7.2 %collective-permute-start.6 = (bf16[2,168,256]{2,1,0:T(8,128)(2,1)S(1)}, bf16[2,168,256]{2,1,0:T(8,128)(2,1)S(1)}, u32[]{:S(2)}, u32[]{:S(2)}) collective-permute-start(bf16[2,168,256]{2,1,0:T(8,128)(2,1)S(1)} %fusion.39), channel_id=1, source_target_pairs={{0,32},{8,40},{16,48},{24,56},{32,64},{40,72},{48,80},{56,88},{64,... | collective-permute-start | bytes 516104 | tf_op jit(solution)/shard_map/ppermute | solution.py:72
  213.4 7.1 %collective-permute-start.13 = (bf16[2,168,256]{2,1,0:T(8,128)(2,1)S(1)}, bf16[2,168,256]{2,1,0:T(8,128)(2,1)S(1)}, u32[]{:S(2)}, u32[]{:S(2)}) collective-permute-start(bf16[2,168,256]{2,1,0:T(8,128)(2,1)S(1)} %fusion.33), channel_id=1, source_target_pairs={{0,224},{8,232},{16,240},{24,248},{32,0},{40,8},{48,16},{56,24},{6... | collective-permute-start | bytes 516104 | tf_op jit(solution)/shard_map/ppermute | solution.py:72
  216.7 6.7 %collective-permute-start.7 = (bf16[2,168,256]{2,1,0:T(8,128)(2,1)S(1)}, bf16[2,168,256]{2,1,0:T(8,128)(2,1)S(1)}, u32[]{:S(2)}, u32[]{:S(2)}) collective-permute-start(bf16[2,168,256]{2,1,0:T(8,128)(2,1)S(1)} %fusion.38), channel_id=1, source_target_pairs={{0,32},{8,40},{16,48},{24,56},{32,64},{40,72},{48,80},{56,88},{64,... | collective-permute-start | bytes 516104 | tf_op jit(solution)/shard_map/ppermute | solution.py:72
  221.5 6.7 %collective-permute-start.14 = (bf16[2,168,256]{2,1,0:T(8,128)(2,1)S(1)}, bf16[2,168,256]{2,1,0:T(8,128)(2,1)S(1)}, u32[]{:S(2)}, u32[]{:S(2)}) collective-permute-start(bf16[2,168,256]{2,1,0:T(8,128)(2,1)S(1)} %fusion.32), channel_id=1, source_target_pairs={{0,224},{8,232},{16,240},{24,248},{32,0},{40,8},{48,16},{56,24},{6... | collective-permute-start | bytes 516104 | tf_op jit(solution)/shard_map/ppermute | solution.py:72
  224.4 6.7 %collective-permute-start.8 = (bf16[2,168,256]{2,1,0:T(8,128)(2,1)S(1)}, bf16[2,168,256]{2,1,0:T(8,128)(2,1)S(1)}, u32[]{:S(2)}, u32[]{:S(2)}) collective-permute-start(bf16[2,168,256]{2,1,0:T(8,128)(2,1)S(1)} %fusion.37), channel_id=1, source_target_pairs={{0,32},{8,40},{16,48},{24,56},{32,64},{40,72},{48,80},{56,88},{64,... | collective-permute-start | bytes 516104 | tf_op jit(solution)/shard_map/ppermute | solution.py:72
  228.3 7.7 %collective-permute-start.15 = (bf16[2,168,256]{2,1,0:T(8,128)(2,1)S(1)}, bf16[2,168,256]{2,1,0:T(8,128)(2,1)S(1)}, u32[]{:S(2)}, u32[]{:S(2)}) collective-permute-start(bf16[2,168,256]{2,1,0:T(8,128)(2,1)S(1)} %fusion.31), channel_id=1, source_target_pairs={{0,224},{8,232},{16,240},{24,248},{32,0},{40,8},{48,16},{56,24},{6... | collective-permute-start | bytes 516104 | tf_op jit(solution)/shard_map/ppermute | solution.py:72
  232.2 26.6 %copy-start.15 = (bf16[128,2,512]{2,0,1:T(8,128)(2,1)S(1)}, bf16[128,2,512]{2,0,1:T(8,128)(2,1)}, u32[]{:S(2)}) copy-start(bf16[128,2,512]{2,0,1:T(8,128)(2,1)} %get-tuple-element.91) | copy-start | bytes 786436
  232.2 6.7 %collective-permute-start.9 = (bf16[2,168,256]{2,1,0:T(8,128)(2,1)S(1)}, bf16[2,168,256]{2,1,0:T(8,128)(2,1)S(1)}, u32[]{:S(2)}, u32[]{:S(2)}) collective-permute-start(bf16[2,168,256]{2,1,0:T(8,128)(2,1)S(1)} %fusion.36), channel_id=1, source_target_pairs={{0,32},{8,40},{16,48},{24,56},{32,64},{40,72},{48,80},{56,88},{64,... | collective-permute-start | bytes 516104 | tf_op jit(solution)/shard_map/ppermute | solution.py:72
  236.0 7.7 %collective-permute-start.16 = (bf16[2,168,256]{2,1,0:T(8,128)(2,1)S(1)}, bf16[2,168,256]{2,1,0:T(8,128)(2,1)S(1)}, u32[]{:S(2)}, u32[]{:S(2)}) collective-permute-start(bf16[2,168,256]{2,1,0:T(8,128)(2,1)S(1)} %fusion.30), channel_id=1, source_target_pairs={{0,224},{8,232},{16,240},{24,248},{32,0},{40,8},{48,16},{56,24},{6... | collective-permute-start | bytes 516104 | tf_op jit(solution)/shard_map/ppermute | solution.py:72
  239.9 6.7 %collective-permute-start.10 = (bf16[2,168,256]{2,1,0:T(8,128)(2,1)S(1)}, bf16[2,168,256]{2,1,0:T(8,128)(2,1)S(1)}, u32[]{:S(2)}, u32[]{:S(2)}) collective-permute-start(bf16[2,168,256]{2,1,0:T(8,128)(2,1)S(1)} %fusion.35), channel_id=1, source_target_pairs={{0,32},{8,40},{16,48},{24,56},{32,64},{40,72},{48,80},{56,88},{64,... | collective-permute-start | bytes 516104 | tf_op jit(solution)/shard_map/ppermute | solution.py:72
  243.7 7.7 %collective-permute-start.17 = (bf16[2,168,256]{2,1,0:T(8,128)(2,1)S(1)}, bf16[2,168,256]{2,1,0:T(8,128)(2,1)S(1)}, u32[]{:S(2)}, u32[]{:S(2)}) collective-permute-start(bf16[2,168,256]{2,1,0:T(8,128)(2,1)S(1)} %fusion.29), channel_id=1, source_target_pairs={{0,224},{8,232},{16,240},{24,248},{32,0},{40,8},{48,16},{56,24},{6... | collective-permute-start | bytes 516104 | tf_op jit(solution)/shard_map/ppermute | solution.py:72
  247.6 6.7 %collective-permute-start.11 = (bf16[2,168,256]{2,1,0:T(8,128)(2,1)S(1)}, bf16[2,168,256]{2,1,0:T(8,128)(2,1)S(1)}, u32[]{:S(2)}, u32[]{:S(2)}) collective-permute-start(bf16[2,168,256]{2,1,0:T(8,128)(2,1)S(1)} %fusion.34), channel_id=1, source_target_pairs={{0,32},{8,40},{16,48},{24,56},{32,64},{40,72},{48,80},{56,88},{64,... | collective-permute-start | bytes 516104 | tf_op jit(solution)/shard_map/ppermute | solution.py:72
  251.4 6.7 %collective-permute-start.18 = (bf16[2,168,256]{2,1,0:T(8,128)(2,1)S(1)}, bf16[2,168,256]{2,1,0:T(8,128)(2,1)S(1)}, u32[]{:S(2)}, u32[]{:S(2)}) collective-permute-start(bf16[2,168,256]{2,1,0:T(8,128)(2,1)S(1)} %fusion.28), channel_id=1, source_target_pairs={{0,224},{8,232},{16,240},{24,248},{32,0},{40,8},{48,16},{56,24},{6... | collective-permute-start | bytes 516104 | tf_op jit(solution)/shard_map/ppermute | solution.py:72
  258.2 5.5 %collective-permute-start.19 = (bf16[168,512]{1,0:T(8,128)(2,1)S(1)}, bf16[168,512]{1,0:T(8,128)(2,1)S(1)}, u32[]{:S(2)}, u32[]{:S(2)}) collective-permute-start(bf16[168,512]{1,0:T(8,128)(2,1)S(1)} %fusion.52), channel_id=1, source_target_pairs={{0,16},{8,24},{16,0},{24,8},{32,48},{40,56},{48,32},{56,40},{64,80... | collective-permute-start | bytes 516104 | tf_op jit(solution)/shard_map/ppermute | solution.py:83
